TPU v7x, 512 devices: a whole 4x4x16 slice. The times are simulated.
512 devices in a mesh: req: 64 (over y_hi, z, core), tp: 8 (over y_lo, x).
Axes of the slice: x: 4, y: 4 (y_hi: 2, y_lo: 2; y = y_hi * 2 + y_lo), z: 16, core: 2. Of those that a mesh axis runs over, the one named last changes fastest.
Arguments:
- tokens: bfloat16 [64, 512, 2048], P('req', 'tp'), may hold values from -6 to 6
- w_q: bfloat16 [2048, 1024], P(None, 'tp')
- w_k: bfloat16 [2048, 1024], P(None, 'tp')
- w_v: bfloat16 [2048, 1024], P(None, 'tp'), may hold values from -0.125 to 0.125
- w_o: bfloat16 [1024, 2048], P('tp'), may hold values from -0.1875 to 0.1875
- q_gain: float32 [1024], P('tp'), may hold values from 0.1 to 1.9
- k_gain: float32 [1024], P('tp'), may hold values from 0.1 to 1.9
- out_gain: float32 [2048], replicated, may hold values from 0.1 to 1.9
- cache_lens: int32 [64], P('req'), may hold values from 512 to 4096, as said below
- group_ids: int32 [64], replicated, may hold values from 0 to 7
- prefix_cache: bfloat16 [8, 1024, 2048], P(None, 'req', 'tp'), may hold values from -6 to 6
- cache_rows: bfloat16 [64, 4096, 2048], P('req', None, 'tp'), may hold values from -105 to 105
Outputs:
- hidden: bfloat16 [64, 512, 2048], P('req', 'tp')
- appended: bfloat16 [64, 512, 2048], P('req', None, 'tp')
Inputs may be any that keep to these rules, and one draw needn't show every extreme that they name: `cache_lens`: every draw holds a request with exactly 4096 cached positions.
All inputs are finite; a program needn't handle non-finite values.
Results may differ from a plain program's by a relative error of at most 0.013.
Values may be sent and summed in bfloat16 or wider, within the bound.
No kernel may reach another device: no remote copies, remote signals or barrier semaphores. Data moves between devices by JAX's collectives and lax.ppermute only.
A program may use at most 64 MiB of HBM per device.

v0:
```python
import jax
import jax.numpy as jnp
from jax import lax
from jax.sharding import PartitionSpec as P

HEADS = 8
HD = 128
NEW = 512


def rotate(values_in, positions):
    half_dim = values_in.shape[-1] // 2
    exponent = jnp.arange(half_dim, dtype=jnp.float32) * (-2.0 / values_in.shape[-1])
    inverse = jnp.power(jnp.float32(500000.0), exponent)
    angles = positions[:, None] * inverse[None, :]
    cosine = jnp.cos(angles)[:, None, :]
    sine_part = jnp.sin(angles)[:, None, :]
    first_half = values_in[..., :half_dim]
    second_half = values_in[..., half_dim:]
    return jnp.concatenate(
        [
            first_half * cosine - second_half * sine_part,
            second_half * cosine + first_half * sine_part,
        ],
        -1,
    )


def rms_scale(values_in, gain_vector):
    mean_sq = jnp.mean(values_in * values_in, axis=-1, keepdims=True)
    return values_in * lax.rsqrt(mean_sq + 1e-06) * gain_vector


def absorb(state_now, queries, keys_block, values_block, visible):
    running_max, denominator, weighted = state_now
    scores = jnp.einsum(
        "hqd,khd->hqk", queries, keys_block, preferred_element_type=jnp.float32
    ) * HD ** (-0.5)
    scores = jnp.where(visible[None], scores, -1e30)
    updated = jnp.maximum(running_max, jnp.max(scores, -1))
    factor = jnp.exp(running_max - updated)
    weights = jnp.where(visible[None], jnp.exp(scores - updated[..., None]), 0.0)
    denominator = denominator * factor + jnp.sum(weights, -1)
    weighted = weighted * factor[..., None] + jnp.einsum(
        "hqk,khd->hqd",
        weights.astype(jnp.bfloat16),
        values_block,
        preferred_element_type=jnp.float32,
    )
    return (updated, denominator, weighted)


def per_device(
    tokens,
    w_q,
    w_k,
    w_v,
    w_o,
    q_gain,
    k_gain,
    out_gain,
    cache_lens,
    group_ids,
    prefix_cache,
    cache_rows,
):
    heads_local = w_q.shape[1] // HD
    width_local = heads_local * HD
    flat_rows = lax.all_gather(tokens, "tp", axis=1, tiled=True)[0]
    projected = jnp.concatenate(
        [
            jnp.dot(flat_rows, w_q, preferred_element_type=jnp.float32)[None],
            jnp.dot(flat_rows, w_k, preferred_element_type=jnp.float32)[None],
            jnp.dot(flat_rows, w_v, preferred_element_type=jnp.float32)[None],
        ],
        axis=2,
    )[0]
    queries = projected[:, :width_local]
    keys_new = projected[:, width_local : 2 * width_local]
    values_new = projected[:, 2 * width_local :]
    square_sums = lax.psum((jnp.sum(queries * queries, -1), jnp.sum(keys_new * keys_new, -1)), "tp")
    full_width = HEADS * HD
    queries = queries * lax.rsqrt(square_sums[0] / full_width + 1e-06)[:, None] * q_gain
    keys_new = keys_new * lax.rsqrt(square_sums[1] / full_width + 1e-06)[:, None] * k_gain
    prefix_len = prefix_cache.shape[1] * lax.axis_size("req")
    length = cache_lens[0]
    positions = (prefix_len + length + jnp.arange(NEW, dtype=jnp.int32)).astype(jnp.float32)
    q_rot = rotate(queries.reshape(NEW, heads_local, HD), positions).astype(jnp.bfloat16)
    k_rot = rotate(keys_new.reshape(NEW, heads_local, HD), positions).astype(jnp.bfloat16)
    v_new = values_new.reshape(NEW, heads_local, HD).astype(jnp.bfloat16)
    appended = jnp.stack([k_rot, v_new], axis=2).reshape(1, NEW, heads_local * 2 * HD)
    q_heads = jnp.transpose(q_rot, (1, 0, 2))
    state_now = (
        jnp.full((heads_local, NEW), -1e30, jnp.float32),
        jnp.zeros((heads_local, NEW), jnp.float32),
        jnp.zeros((heads_local, NEW, HD), jnp.float32),
    )
    row_ids = jnp.arange(NEW, dtype=jnp.int32)
    state_now = absorb(state_now, q_heads, k_rot, v_new, row_ids[None, :] <= row_ids[:, None])
    cached = cache_rows[0]
    key_block = min(512, cached.shape[0])

    def cache_step(block_index, state_in):
        block = lax.dynamic_slice_in_dim(cached, block_index * key_block, key_block, 0).reshape(
            key_block, heads_local, 2, HD
        )
        columns = block_index * key_block + jnp.arange(key_block, dtype=jnp.int32)
        visible = jnp.broadcast_to(columns[None, :] < length, (NEW, key_block))
        return absorb(state_in, q_heads, block[:, :, 0], block[:, :, 1], visible)

    block_count = cached.shape[0] // key_block
    state_now = lax.fori_loop(0, block_count, cache_step, state_now)
    group_id = group_ids[lax.axis_index("req")]
    chosen = lax.dynamic_index_in_dim(
        lax.all_gather(prefix_cache, "req", axis=1, tiled=True), group_id, 0, keepdims=False
    )
    count = chosen.shape[0]
    chosen = chosen.reshape(count, heads_local, 2, HD)
    state_now = absorb(
        state_now, q_heads, chosen[:, :, 0], chosen[:, :, 1], jnp.ones((NEW, count), dtype=bool)
    )
    running_max, denominator, weighted = state_now
    attended = (
        jnp.transpose(weighted / denominator[..., None], (1, 0, 2))
        .reshape(NEW, width_local)
        .astype(jnp.bfloat16)
    )
    partial_out = jnp.dot(attended, w_o, preferred_element_type=jnp.float32)
    share_rows = tokens.shape[1]
    summed = lax.psum(partial_out.astype(jnp.bfloat16), "tp").astype(jnp.float32)
    mine = lax.dynamic_slice_in_dim(summed, lax.axis_index("tp") * share_rows, share_rows, 0)
    hidden = (tokens[0].astype(jnp.float32) + rms_scale(mine, out_gain)).astype(jnp.bfloat16)[None]
    return (hidden, appended)


def solution(mesh):
    return jax.shard_map(
        per_device,
        mesh=mesh,
        in_specs=(
            P("req", "tp", None),
            P(None, "tp"),
            P(None, "tp"),
            P(None, "tp"),
            P("tp", None),
            P("tp"),
            P("tp"),
            P(),
            P("req"),
            P(),
            P(None, "req", "tp"),
            P("req", None, "tp"),
        ),
        out_specs=(P("req", "tp", None), P("req", None, "tp")),
        check_vma=False,
    )
```

profile of v0, /device:TPU:1, one launch (start us, length us, event | category | flops | bytes accessed | tf_op | source)
XLA Modules:
  0.0 325.5 jit_solution(8489403628430038322)
XLA Ops:
  7.2 0.7 all-gather.3.cloned.1.call-update
  8.0 1.5 copy.30
  10.2 3.0 copy.28
  15.8 43.2 %all-gather.3.cloned.1.call-done = bf16[1,512,2048]{2,1,0:T(8,128)(2,1)} async-done(((bf16[1,64,2048]{2,1,0:T(8,128)(2,1)}), bf16[1,512,2048]{2,1,0:T(8,128)(2,1)}) %all-gather.3.cloned.1.call-update) | async-done | bytes 2097168 | tf_op jit(solution)/shard_map/all_gather | solution.py:69
  58.9 2.6 fusion.19
  61.5 0.8 fusion.22
  62.6 0.8 fusion.25
  63.5 14.7 %all-reduce = (f32[512]{0:T(512)S(1)}, f32[512]{0:T(512)S(1)}) all-reduce(f32[512]{0:T(512)S(1)} %get-tuple-element.168, f32[512]{0:T(512)S(1)} %get-tuple-element.167), channel_id=1, replica_groups=mesh['req'=64,'tp'=8] {'tp'}, use_global_device_ids=true, to_apply=%region_1.0 | all-reduce | flops 1024 | bytes 8192 | tf_op jit(solution)/shard_map/psum | solution.py:81
  78.4 1.3 fusion.63
  80.3 1.5 pad_maximum_fusion.2
  81.8 1.0 copy.29
  82.8 1.3 fusion.78
  84.3 1.3 fusion.28
  85.6 15.0 %while.17 = (s32[]{:T(128)}, f32[1,512]{1,0:T(1,128)S(1)}, f32[1,512]{1,0:T(1,128)S(1)}, f32[1,512,128]{2,1,0:T(8,128)S(1)}, s32[]{:T(128)}, /*index=5*/bf16[409...) while((s32[]{:T(128)}, f32[1,512]{1,0:T(1,128)S(1)}, ...), condition=%wide.region_9.10_spmd, body=%wide.region_6.9_spmd.sunk | while | flops 136710144 | bytes 4622503 | solution.py:112
  100.6 118.5 %all-gather.5.cloned.1.call-done = bf16[8,1024,256]{2,0,1:T(8,128)(2,1)} async-done(((bf16[8,16,256]{2,0,1:T(8,128)(2,1)}), bf16[8,1024,256]{2,0,1:T(8,128)(2,1)}) %all-gather.5.cloned.1.call-update) | async-done | bytes 4194320 | tf_op jit(solution)/shard_map/all_gather | solution.py:115
  219.1 3.3 %constant_dynamic-slice_fusion.1 = bf16[1,1024,256]{2,0,1:T(2,128)(2,1)S(1)} fusion(bf16[8,1024,256]{2,0,1:T(8,128)(2,1)} %all-gather.5.cloned.1.call-done, s32[]{:T(128)S(6)} %select_n.49), kind=kLoop, calls=%fused_computation.103 | loop fusion | bytes 1048580 | tf_op jit(solution)/shard_map/jit(dynamic_index_in_dim)/dynamic_slice | solution.py:114
  222.4 1.3 copy.35
  223.7 1.4 multiply_reduce_fusion
  225.6 2.4 convolution_convert_fusion
  228.1 1.0 fusion.71
  229.2 0.8 copy.34
  230.0 86.0 %all-reduce.3.cloned.1.call-done = bf16[512,2048]{1,0:T(8,128)(2,1)} async-done(((bf16[512,2048]{1,0:T(8,128)(2,1)}), bf16[512,2048]{1,0:T(8,128)(2,1)}) %all-reduce.3.cloned.1.call-update) | async-done | bytes 2097168 | tf_op jit(solution)/shard_map/psum | solution.py:130
  316.0 1.1 fusion.43
  317.1 1.8 fusion.47
  (114 shorter events, 17.1 us)
Async XLA Ops:
  7.2 218.5 %copy-start = (bf16[128,2048]{1,0:T(8,128)(2,1)S(1)}, bf16[128,2048]{1,0:T(8,128)(2,1)}, u32[]{:S(2)}) copy-start(bf16[128,2048]{1,0:T(8,128)(2,1)} %param.18) | copy-start | bytes 1572868
  7.2 51.8 %all-gather.3.cloned.1.call-start = ((), (), s32[]{:S(2)}) async-start(), calls=%async_computation | async-start | bytes 2359296 | tf_op jit(solution)/shard_map/all_gather | solution.py:69
  7.9 211.2 %all-gather.5.cloned.1.call-start = ((), (), s32[]{:S(2)}) async-start(), calls=%async_computation.1 | async-start | bytes 4259840 | tf_op jit(solution)/shard_map/all_gather | solution.py:115
  9.5 306.5 %all-reduce.3.cloned.1.call-start = ((), (), s32[]{:S(2)}) async-start(), calls=%async_computation.2 | async-start | bytes 4194304 | tf_op jit(solution)/shard_map/psum | solution.py:130
  10.2 3.0 copy-start.14
  10.2 48.7 %copy-start.6 = (bf16[2048,128]{1,0:T(8,128)(2,1)S(1)}, bf16[2048,128]{1,0:T(8,128)(2,1)}, u32[]{:S(2)}) copy-start(bf16[2048,128]{1,0:T(8,128)(2,1)} %param.15) | copy-start | bytes 1572868
  58.9 2.6 copy-start.1
  58.9 2.6 copy-start.7
  61.5 1.0 copy-start.8
  62.6 15.7 %copy-start.12 = (f32[128]{0:T(128)S(1)}, f32[128]{0:T(128)}, u32[]{:S(2)}) copy-start(f32[128]{0:T(128)} %param.20) | copy-start | bytes 1540
  62.6 15.7 %copy-start.13 = (f32[128]{0:T(128)S(1)}, f32[128]{0:T(128)}, u32[]{:S(2)}) copy-start(f32[128]{0:T(128)} %param.19) | copy-start | bytes 1540
  63.5 20.6 %copy-start.2 = (f32[512,384]{0,1:T(8,128)}, f32[512,384]{0,1:T(8,128)S(1)}, u32[]{:S(2)}) copy-start(f32[512,384]{0,1:T(8,128)S(1)} %maximum_bitcast_fusion) | copy-start | bytes 2359300
  79.6 0.6 copy-start.4
  100.6 123.1 %copy-start.5 = (bf16[512,1,64]{0,2,1:T(8,128)(2,1)S(1)}, bf16[512,1,64]{0,2,1:T(8,128)(2,1)}, u32[]{:S(2)}) copy-start(bf16[512,1,64]{0,2,1:T(8,128)(2,1)} %copy-done.4) | copy-start | bytes 196612
  228.1 1.1 copy-start.9
  228.1 1.1 copy-start.10
  228.1 89.0 %copy-start.3 = (bf16[1,64,2048]{2,1,0:T(8,128)(2,1)S(1)}, bf16[1,64,2048]{2,1,0:T(8,128)(2,1)}, u32[]{:S(2)}) copy-start(bf16[1,64,2048]{2,1,0:T(8,128)(2,1)} %param.14) | copy-start | bytes 786436
  228.1 89.0 %copy-start.11 = (f32[2048]{0:T(1024)S(1)}, f32[2048]{0:T(1024)}, u32[]{:S(2)}) copy-start(f32[2048]{0:T(1024)} %param.21) | copy-start | bytes 24580
Sparse Core Ops, SparseCore 0:
  10.1 48.8 all-gather.2
  62.8 156.2 all-gather.4
  228.2 87.7 all-reduce.2
where the time goes:
time: 329 us; the launch traced here: 325 us
  waiting for transfers between devices  248 us (75%)
  matrix products  17.8 us (5%)
  between operations  16.6 us (5%)
  blocking collectives  14.7 us (4%)
  other arithmetic  13.8 us (4%)
  local copies, waits for them, and re-layouts  13.6 us (4%)
    all_gather x1, waiting for transfers between devices, per_device(): lax.all_gather(prefix_cache, 'req', axis=1, tiled=True)  119 us
    psum x1, waiting for transfers between devices, per_device(): lax.psum(partial_out.astype(jnp.bfloat16), 'tp').astype(jnp.float32)  86 us
    all_gather x1, waiting for transfers between devices, per_device(): flat_rows = lax.all_gather(tokens, 'tp', axis=1, tiled=True)[0]  43.2 us
    psum x1, blocking collectives, per_device(): lax.psum((jnp.sum(queries * queries, -1), jnp.sum(keys_new * keys_new, -1...  14.7 us
    unnamed x34, local copies, waits for them, and re-layouts  7.52 us
  transfers between devices with their start and end apart: 3, of which 3 were waited for; matrix products, arithmetic and copies ran while one was open for 10% of the time, Pallas kernels for 0%

commit v1 on v0

--- a/solution.py
+++ b/solution.py
@@ -110,10 +110,8 @@
 
     block_count = cached.shape[0] // key_block
     state_now = lax.fori_loop(0, block_count, cache_step, state_now)
-    group_id = group_ids[lax.axis_index("req")]
-    chosen = lax.dynamic_index_in_dim(
-        lax.all_gather(prefix_cache, "req", axis=1, tiled=True), group_id, 0, keepdims=False
-    )
+    outgoing = jnp.take(prefix_cache, group_ids, axis=0)
+    chosen = lax.all_to_all(outgoing, "req", 0, 0, tiled=True).reshape(-1, prefix_cache.shape[2])
     count = chosen.shape[0]
     chosen = chosen.reshape(count, heads_local, 2, HD)
     state_now = absorb(
@@ -126,9 +124,9 @@
         .astype(jnp.bfloat16)
     )
     partial_out = jnp.dot(attended, w_o, preferred_element_type=jnp.float32)
-    share_rows = tokens.shape[1]
-    summed = lax.psum(partial_out.astype(jnp.bfloat16), "tp").astype(jnp.float32)
-    mine = lax.dynamic_slice_in_dim(summed, lax.axis_index("tp") * share_rows, share_rows, 0)
+    mine = lax.psum_scatter(
+        partial_out.astype(jnp.bfloat16), "tp", scatter_dimension=0, tiled=True
+    ).astype(jnp.float32)
     hidden = (tokens[0].astype(jnp.float32) + rms_scale(mine, out_gain)).astype(jnp.bfloat16)[None]
     return (hidden, appended)
 

time: 329 us -> 173 us (0.53)
  the two profiles are of different devices: /device:TPU:1 before, /device:TPU:32 now
where the time goes in v1:
time: 173 us; the launch traced here: 172 us
  waiting for transfers between devices  74.6 us (43%)
  blocking collectives  18.8 us (11%)
  starting transfers between devices  18.7 us (11%)
  matrix products  18.2 us (11%)
  other arithmetic  15.2 us (9%)
  between operations  14.9 us (9%)
  local copies, waits for them, and re-layouts  11.2 us (6%)
    reduce_scatter x1, waiting for transfers between devices, per_device(): lax.psum_scatter(partial_out.astype(jnp.bfloat16), 'tp', scatter_dimensio...  45.1 us
    all_to_all x1, waiting for transfers between devices, per_device(): lax.all_to_all(outgoing, 'req', 0, 0, tiled=True)  28.8 us
    psum x1, blocking collectives, per_device(): lax.psum((jnp.sum(queries * queries, -1), jnp.sum(keys_new * keys_new, -1...  18.8 us
    all_to_all x1, starting transfers between devices, per_device(): lax.all_to_all(outgoing, 'req', 0, 0, tiled=True)  18.6 us
    dot_general x10, matrix products, absorb(): jnp.einsum('hqd,khd->hqk', queries, keys_block, preferred_element_type=jn...  5.77 us
    dot_general x9, matrix products, absorb(): jnp.einsum('hqk,khd->hqd', weights.astype(jnp.bfloat16), values_block, pr...  5.68 us
    lt x8, other arithmetic, cache_step(): visible = jnp.broadcast_to(columns[None, :] < length, (NEW, key_block))  5.23 us
    unnamed x30, local copies, waits for them, and re-layouts  4.65 us
  transfers between devices with their start and end apart: 3, of which 2 were waited for; matrix products, arithmetic and copies ran while one was open for 7% of the time, Pallas kernels for 0%

profile of v1, /device:TPU:32, one launch (start us, length us, event | category | flops | bytes accessed | tf_op | source)
XLA Modules:
  0.0 172.1 jit_solution(3037785717470526430)
XLA Ops:
  7.2 0.7 all-gather.2.cloned.1.call-update
  8.6 1.4 gather_fusion
  10.7 0.9 broadcast_select_fusion
  11.6 18.6 %all-to-all-start = ((bf16[64,16,256]{2,1,0:T(8,128)(2,1)}), bf16[64,16,256]{2,1,0:T(8,128)(2,1)}, u32[]{:S(2)}, u32[]{:S(2)}) async-start(bf16[64,16,256]{2,1,0:T(8,128)(2,1)} %broadcast_select_fusion), calls=%async_computation | async-start | bytes 1048576 | tf_op jit(solution)/shard_map/all_to_all | solution.py:114
  30.9 2.9 %copy.20 = bf16[1,4096,256]{1,2,0:T(8,128)(2,1)S(1)} copy(bf16[1,4096,256]{2,1,0:T(8,128)(2,1)} %param.25) | data formatting | bytes 4194304 | tf_op args[11]
  33.9 28.8 %all-to-all-done = bf16[64,16,256]{2,1,0:T(8,128)(2,1)} async-done(((bf16[64,16,256]{2,1,0:T(8,128)(2,1)}), bf16[64,16,256]{2,1,0:T(8,128)(2,1)}, u32[]{:S(2)}, u32[]{:S(2)}) %all-to-all-start) | async-done | bytes 524320 | tf_op jit(solution)/shard_map/all_to_all | solution.py:114
  62.6 1.2 reshape_reshape.3
  63.8 1.7 fusion.84
  65.5 2.6 %fusion.19 = f32[1,512,128]{1,2,0:T(8,128)S(1)} fusion(bf16[2048,128]{1,0:T(8,128)(2,1)} %param.15, bf16[1,512,2048]{2,1,0:T(8,128)(2,1)} %all-gather.2.cloned.1.call-done), kind=kOutput, calls=%fused_computation.32 | convolution fusion | flops 268435456 | bytes 2883584 | tf_op jit(solution)/shard_map/dot_general | solution.py:72
  68.2 0.8 fusion.22
  69.2 0.8 fusion.25
  70.2 18.8 %all-reduce = (f32[512]{0:T(512)S(1)}, f32[512]{0:T(512)S(1)}) all-reduce(f32[512]{0:T(512)S(1)} %get-tuple-element.159, f32[512]{0:T(512)S(1)} %get-tuple-element.158), channel_id=1, replica_groups=mesh['req'=64,'tp'=8] {'tp'}, use_global_device_ids=true, to_apply=%region_1.0 | all-reduce | flops 1024 | bytes 8192 | tf_op jit(solution)/shard_map/psum | solution.py:81
  89.1 1.2 fusion.69
  91.7 1.0 copy.21
  92.7 1.3 fusion.85
  94.2 1.3 fusion.28
  95.5 15.0 %while.17 = (s32[]{:T(128)}, f32[1,512]{1,0:T(1,128)S(1)}, f32[1,512]{1,0:T(1,128)S(1)}, f32[1,512,128]{2,1,0:T(8,128)S(1)}, s32[]{:T(128)}, /*index=5*/bf16[409...) while((s32[]{:T(128)}, f32[1,512]{1,0:T(1,128)S(1)}, ...), condition=%wide.region_9.10_spmd, body=%wide.region_6.9_spmd.sunk | while | flops 136710144 | bytes 4622503 | solution.py:112
  110.5 1.7 multiply_reduce_fusion
  112.8 2.5 %convolution_convert_fusion = bf16[512,2048]{1,0:T(8,128)(2,1)} fusion(bf16[128,2048]{1,0:T(8,128)(2,1)S(1)} %copy-done, f32[512,1024]{1,0:T(8,128)S(1)} %get-tuple-element.197, f32[512]{0:T(512)S(1)} %bitcast.146, bf16[1024,1,1,128]{3,2,0,1:T(2,128)(2,1)S(1)} %copy-done.3, f32[1,512,128]{2,1,0:T(8,128)S(1)} %get-tuple-element.128, f32[512]{0:T(512)S(1)} %bitcast.148, ...), kind=kOutput, calls=%fused_computation.19 | convolution fusion | flops 405536768 | bytes 5249024 | tf_op jit(solution)/shard_map/dot_general | solution.py:126
  115.3 1.0 fusion.77
  116.3 0.8 copy.22
  117.2 45.1 %reduce-scatter.2.cloned.1.call-done = bf16[64,2048]{1,0:T(8,128)(2,1)} async-done(((bf16[512,2048]{1,0:T(8,128)(2,1)}), bf16[64,2048]{1,0:T(8,128)(2,1)}) %reduce-scatter.2.cloned.1.call-update) | async-done | bytes 262160 | tf_op jit(solution)/shard_map/reduce_scatter | solution.py:127
  162.3 1.1 fusion.40
  163.4 1.8 %fusion.47 = bf16[1,64,2048]{2,1,0:T(8,128)(2,1)} fusion(bf16[64,2048]{1,0:T(8,128)(2,1)} %reduce-scatter.2.cloned.1.call-done, bf16[1,64,2048]{2,1,0:T(8,128)(2,1)S(1)} %copy-done.4, f32[2048]{0:T(1024)S(1)} %copy-done.11, f32[64]{0:T(128)S(1)} %add_rsqrt_fusion.2), kind=kLoop, calls=%fused_computation.58 | loop fusion | flops 786432 | bytes 794880 | tf_op jit(solution)/shard_map/broadcast_in_dim | solution.py:130
  (114 shorter events, 18.4 us)
Async XLA Ops:
  7.2 105.6 %copy-start = (bf16[128,2048]{1,0:T(8,128)(2,1)S(1)}, bf16[128,2048]{1,0:T(8,128)(2,1)}, u32[]{:S(2)}) copy-start(bf16[128,2048]{1,0:T(8,128)(2,1)} %param.18) | copy-start | bytes 1572868
  7.2 58.3 %all-gather.2.cloned.1.call-start = ((), (), s32[]{:S(2)}) async-start(), calls=%async_computation.2 | async-start | bytes 2359296 | tf_op jit(solution)/shard_map/all_gather | solution.py:69
  11.6 51.0 %all-to-all-start = ((bf16[64,16,256]{2,1,0:T(8,128)(2,1)}), bf16[64,16,256]{2,1,0:T(8,128)(2,1)}, u32[]{:S(2)}, u32[]{:S(2)}) async-start(bf16[64,16,256]{2,1,0:T(8,128)(2,1)} %broadcast_select_fusion), calls=%async_computation | async-start | bytes 1048576 | tf_op jit(solution)/shard_map/all_to_all | solution.py:114
  30.2 132.1 %reduce-scatter.2.cloned.1.call-start = ((), (), s32[]{:S(2)}) async-start(), calls=%async_computation.3 | async-start | bytes 2359296 | tf_op jit(solution)/shard_map/reduce_scatter | solution.py:127
  65.5 2.7 %copy-start.7 = (bf16[2048,128]{1,0:T(8,128)(2,1)S(1)}, bf16[2048,128]{1,0:T(8,128)(2,1)}, u32[]{:S(2)}) copy-start(bf16[2048,128]{1,0:T(8,128)(2,1)} %param.16) | copy-start | bytes 1572868
  65.5 2.7 %copy-start.1 = (bf16[1,512,2048]{2,1,0:T(8,128)(2,1)S(1)}, bf16[1,512,2048]{2,1,0:T(8,128)(2,1)}, u32[]{:S(2)}) copy-start(bf16[1,512,2048]{2,1,0:T(8,128)(2,1)} %all-gather.2.cloned.1.call-done) | copy-start | bytes 6291460
  68.2 1.0 copy-start.8
  69.2 19.8 %copy-start.12 = (f32[128]{0:T(128)S(1)}, f32[128]{0:T(128)}, u32[]{:S(2)}) copy-start(f32[128]{0:T(128)} %param.20) | copy-start | bytes 1540
  69.2 19.8 %copy-start.13 = (f32[128]{0:T(128)S(1)}, f32[128]{0:T(128)}, u32[]{:S(2)}) copy-start(f32[128]{0:T(128)} %param.19) | copy-start | bytes 1540
  70.1 23.9 %copy-start.2 = (f32[512,384]{0,1:T(8,128)}, f32[512,384]{0,1:T(8,128)S(1)}, u32[]{:S(2)}) copy-start(f32[512,384]{0,1:T(8,128)S(1)} %maximum_bitcast_fusion) | copy-start | bytes 2359300
  90.4 0.6 copy-start.5
  90.4 0.6 copy-start.6
  110.5 2.3 %copy-start.3 = (bf16[1024,1,1,128]{3,2,0,1:T(2,128)(2,1)S(1)}, bf16[1024,1,1,128]{3,2,0,1:T(2,128)(2,1)}, u32[]{:S(2)}) copy-start(bf16[1024,1,1,128]{3,2,0,1:T(2,128)(2,1)} %get-tuple-element.184) | copy-start | bytes 786436
  115.2 1.1 copy-start.9
  115.2 1.1 copy-start.10
  115.2 48.2 %copy-start.4 = (bf16[1,64,2048]{2,1,0:T(8,128)(2,1)S(1)}, bf16[1,64,2048]{2,1,0:T(8,128)(2,1)}, u32[]{:S(2)}) copy-start(bf16[1,64,2048]{2,1,0:T(8,128)(2,1)} %param.14) | copy-start | bytes 786436
  115.2 48.2 %copy-start.11 = (f32[2048]{0:T(1024)S(1)}, f32[2048]{0:T(1024)}, u32[]{:S(2)}) copy-start(f32[2048]{0:T(1024)} %param.21) | copy-start | bytes 24580
Sparse Core Ops, SparseCore 0:
  10.1 53.6 all-gather.1
  115.4 46.8 reduce-scatter.1

commit v2 on v1

--- a/solution.py
+++ b/solution.py
@@ -66,7 +66,10 @@
 ):
     heads_local = w_q.shape[1] // HD
     width_local = heads_local * HD
-    flat_rows = lax.all_gather(tokens, "tp", axis=1, tiled=True)[0]
+    tp_size = lax.axis_size("tp")
+    flat_rows = lax.all_to_all(
+        jnp.broadcast_to(tokens, (tp_size,) + tokens.shape[1:]), "tp", 0, 0, tiled=True
+    ).reshape(-1, tokens.shape[2])
     projected = jnp.concatenate(
         [
             jnp.dot(flat_rows, w_q, preferred_element_type=jnp.float32)[None],
@@ -124,9 +127,8 @@
         .astype(jnp.bfloat16)
     )
     partial_out = jnp.dot(attended, w_o, preferred_element_type=jnp.float32)
-    mine = lax.psum_scatter(
-        partial_out.astype(jnp.bfloat16), "tp", scatter_dimension=0, tiled=True
-    ).astype(jnp.float32)
+    blocks = partial_out.astype(jnp.bfloat16).reshape(tp_size, -1, partial_out.shape[1])
+    mine = jnp.sum(lax.all_to_all(blocks, "tp", 0, 0, tiled=True).astype(jnp.float32), 0)
     hidden = (tokens[0].astype(jnp.float32) + rms_scale(mine, out_gain)).astype(jnp.bfloat16)[None]
     return (hidden, appended)
 

time: 173 us -> 138 us (0.80)
  the two profiles are of different devices: /device:TPU:32 before, /device:TPU:1 now
where the time goes in v2:
time: 138 us
  waiting for transfers between devices  45.9 us (33%)
  starting transfers between devices  28.4 us (21%)
  local copies, waits for them, and re-layouts  18.1 us (13%)
  blocking collectives  17.6 us (13%)
  matrix products  14.5 us (11%)
  other arithmetic  11 us (8%)
  between operations  1.62 us (1%)
    all_to_all x1, waiting for transfers between devices, per_device(): lax.all_to_all(blocks, 'tp', 0, 0, tiled=True).astype(jnp.float32)  25.2 us
    all_to_all x1, waiting for transfers between devices, per_device(): lax.all_to_all(jnp.broadcast_to(tokens, (tp_size,) + tokens.shape[1:]), '...  20.7 us
    all_to_all x1, starting transfers between devices, per_device(): lax.all_to_all(outgoing, 'req', 0, 0, tiled=True)  18.8 us
    psum x1, blocking collectives, per_device(): lax.psum((jnp.sum(queries * queries, -1), jnp.sum(keys_new * keys_new, -1...  17.6 us
    dynamic_slice x8, local copies, waits for them, and re-layouts, cache_step(): lax.dynamic_slice_in_dim(cached, block_index * key_block, key_block, 0)  7.79 us
    all_to_all x1, starting transfers between devices, per_device(): lax.all_to_all(jnp.broadcast_to(tokens, (tp_size,) + tokens.shape[1:]), '...  5.85 us
    unnamed x30, local copies, waits for them, and re-layouts  5.23 us
    lt x8, other arithmetic, cache_step(): visible = jnp.broadcast_to(columns[None, :] < length, (NEW, key_block))  5.23 us
  transfers between devices with their start and end apart: 3, of which 2 were waited for; matrix products, arithmetic and copies ran while one was open for 26% of the time, Pallas kernels for 0%

profile of v2, /device:TPU:1, one launch (start us, length us, event | category | flops | bytes accessed | tf_op | source)
XLA Modules:
  0.0 137.5 jit_solution(6727066951137875178)
XLA Ops:
  0.6 2.6 %broadcast_in_dim.109 = bf16[8,64,2048]{2,1,0:T(8,128)(2,1)} broadcast(bf16[64,2048]{1,0:T(8,128)(2,1)} %bitcast.129), dimensions={1,2} | broadcast | bytes 2359296 | tf_op jit(solution)/shard_map/broadcast_in_dim | solution.py:71
  3.2 5.9 %all-to-all-start = ((bf16[8,64,2048]{2,1,0:T(8,128)(2,1)}), bf16[8,64,2048]{2,1,0:T(8,128)(2,1)S(1)}, u32[]{:S(2)}, u32[]{:S(2)}) async-start(bf16[8,64,2048]{2,1,0:T(8,128)(2,1)} %broadcast_in_dim.109), calls=%async_computation | async-start | bytes 4194304 | tf_op jit(solution)/shard_map/all_to_all | solution.py:70
  9.7 4.1 %copy.20 = bf16[1,4096,256]{1,2,0:T(8,128)(2,1)} copy(bf16[1,4096,256]{2,1,0:T(8,128)(2,1)} %param.25) | data formatting | bytes 4194304 | tf_op args[11]
  14.5 0.9 broadcast_select_fusion
  15.5 20.7 %all-to-all-done = bf16[8,64,2048]{2,1,0:T(8,128)(2,1)S(1)} async-done(((bf16[8,64,2048]{2,1,0:T(8,128)(2,1)}), bf16[8,64,2048]{2,1,0:T(8,128)(2,1)S(1)}, u32[]{:S(2)}, u32[]{:S(2)}) %all-to-all-start) | async-done | bytes 2097184 | tf_op jit(solution)/shard_map/all_to_all | solution.py:70
  36.2 18.8 %all-to-all-start.1 = ((bf16[64,16,256]{2,1,0:T(8,128)(2,1)}), bf16[64,16,256]{2,1,0:T(8,128)(2,1)S(1)}, u32[]{:S(2)}, u32[]{:S(2)}) async-start(bf16[64,16,256]{2,1,0:T(8,128)(2,1)} %broadcast_select_fusion), calls=%async_computation.1 | async-start | bytes 1048576 | tf_op jit(solution)/shard_map/all_to_all | solution.py:117
  55.0 1.9 %convolution_bitcast_fusion.1 = f32[1,512,128]{1,2,0:T(8,128)S(1)} fusion(bf16[512,2048]{1,0:T(8,128)(2,1)S(1)} %bitcast.120, bf16[2048,128]{1,0:T(8,128)(2,1)} %param.17), kind=kOutput, calls=%fused_computation.29 | convolution fusion | flops 268435456 | bytes 2883584 | tf_op jit(solution)/shard_map/dot_general | solution.py:77
  56.9 0.8 convolution_bitcast_fusion.2
  58.9 17.6 %all-reduce = (f32[512]{0:T(512)S(1)}, f32[512]{0:T(512)S(1)}) all-reduce(f32[512]{0:T(512)S(1)} %get-tuple-element.159, f32[512]{0:T(512)S(1)} %get-tuple-element.158), channel_id=1, replica_groups=mesh['req'=64,'tp'=8] {'tp'}, use_global_device_ids=true, to_apply=%region_1.0 | all-reduce | flops 1024 | bytes 8192 | tf_op jit(solution)/shard_map/psum | solution.py:84
  78.3 22.6 %while.17 = (s32[]{:T(128)}, f32[1,512]{1,0:T(1,128)S(1)}, f32[1,512]{1,0:T(1,128)S(1)}, f32[1,512,128]{2,1,0:T(8,128)S(1)}, s32[]{:T(128)}, /*index=5*/bf16[409...) while((s32[]{:T(128)}, f32[1,512]{1,0:T(1,128)S(1)}, ...), condition=%wide.region_9.10_spmd, body=%wide.region_6.9_spmd.sunk | while | flops 136710144 | bytes 4622503 | solution.py:115
  78.3 1.0 constant_dynamic-slice_fusion.2
  81.1 1.0 constant_dynamic-slice_fusion.2
  84.0 1.0 constant_dynamic-slice_fusion.2
  86.8 1.0 constant_dynamic-slice_fusion.2
  89.6 1.0 constant_dynamic-slice_fusion.2
  92.4 1.0 constant_dynamic-slice_fusion.2
  95.2 1.0 constant_dynamic-slice_fusion.2
  98.1 1.0 constant_dynamic-slice_fusion.2
  102.9 2.5 %convolution_convert_fusion = bf16[512,2048]{1,0:T(8,128)(2,1)} fusion(bf16[128,2048]{1,0:T(8,128)(2,1)S(1)} %copy-done, f32[512,1024]{1,0:T(8,128)S(1)} %get-tuple-element.197, f32[512]{0:T(512)S(1)} %bitcast.147, bf16[1024,1,1,128]{3,2,0,1:T(2,128)(2,1)S(1)} %get-tuple-element.184, f32[1,512,128]{2,1,0:T(8,128)S(1)} %get-tuple-element.128, ...), kind=kOutput, calls=%fused_computation.20 | convolution fusion | flops 405536768 | bytes 5249024 | tf_op jit(solution)/shard_map/dot_general | solution.py:129
  105.3 3.7 %all-to-all-start.2 = ((bf16[8,64,2048]{2,1,0:T(8,128)(2,1)}), bf16[8,64,2048]{2,1,0:T(8,128)(2,1)S(1)}, u32[]{:S(2)}, u32[]{:S(2)}) async-start(bf16[8,64,2048]{2,1,0:T(8,128)(2,1)} %bitcast.125), calls=%async_computation.2 | async-start | bytes 4194304 | tf_op jit(solution)/shard_map/all_to_all | solution.py:131
  109.1 1.0 fusion.60
  110.1 0.8 copy.22
  111.0 25.2 %all-to-all-done.2 = bf16[8,64,2048]{2,1,0:T(8,128)(2,1)S(1)} async-done(((bf16[8,64,2048]{2,1,0:T(8,128)(2,1)}), bf16[8,64,2048]{2,1,0:T(8,128)(2,1)S(1)}, u32[]{:S(2)}, u32[]{:S(2)}) %all-to-all-start.2) | async-done | bytes 2097184 | tf_op jit(solution)/shard_map/all_to_all | solution.py:131
  136.6 0.9 fusion.28
  (114 shorter events, 20.4 us)
Async XLA Ops:
  0.6 102.2 %copy-start = (bf16[128,2048]{1,0:T(8,128)(2,1)S(1)}, bf16[128,2048]{1,0:T(8,128)(2,1)}, u32[]{:S(2)}) copy-start(bf16[128,2048]{1,0:T(8,128)(2,1)} %param.18) | copy-start | bytes 1572868
  3.2 33.0 %all-to-all-start = ((bf16[8,64,2048]{2,1,0:T(8,128)(2,1)}), bf16[8,64,2048]{2,1,0:T(8,128)(2,1)S(1)}, u32[]{:S(2)}, u32[]{:S(2)}) async-start(bf16[8,64,2048]{2,1,0:T(8,128)(2,1)} %broadcast_in_dim.109), calls=%async_computation | async-start | bytes 4194304 | tf_op jit(solution)/shard_map/all_to_all | solution.py:70
  9.7 4.1 %copy-start.13 = (s32[64]{0:T(128)S(1)}, s32[64]{0:T(128)}, u32[]{:S(2)}) copy-start(s32[64]{0:T(128)} %param.23) | copy-start | bytes 772
  9.7 4.2 %copy-start.2 = (bf16[8,16,256]{2,1,0:T(8,128)(2,1)S(1)}, bf16[8,16,256]{2,1,0:T(8,128)(2,1)}, u32[]{:S(2)}) copy-start(bf16[8,16,256]{2,1,0:T(8,128)(2,1)} %param.24) | copy-start | bytes 196612
  36.2 64.7 %all-to-all-start.1 = ((bf16[64,16,256]{2,1,0:T(8,128)(2,1)}), bf16[64,16,256]{2,1,0:T(8,128)(2,1)S(1)}, u32[]{:S(2)}, u32[]{:S(2)}) async-start(bf16[64,16,256]{2,1,0:T(8,128)(2,1)} %broadcast_select_fusion), calls=%async_computation.1 | async-start | bytes 1048576 | tf_op jit(solution)/shard_map/all_to_all | solution.py:117
  54.9 1.9 %copy-start.4 = (bf16[2048,128]{1,0:T(8,128)(2,1)S(1)}, bf16[2048,128]{1,0:T(8,128)(2,1)}, u32[]{:S(2)}) copy-start(bf16[2048,128]{1,0:T(8,128)(2,1)} %param.16) | copy-start | bytes 1572868
  56.9 1.0 copy-start.5
  57.9 18.5 %copy-start.11 = (f32[128]{0:T(128)S(1)}, f32[128]{0:T(128)}, u32[]{:S(2)}) copy-start(f32[128]{0:T(128)} %param.20) | copy-start | bytes 1540
  57.9 18.5 %copy-start.12 = (f32[128]{0:T(128)S(1)}, f32[128]{0:T(128)}, u32[]{:S(2)}) copy-start(f32[128]{0:T(128)} %param.19) | copy-start | bytes 1540
  58.8 19.1 %copy-start.1 = (f32[512,384]{0,1:T(8,128)}, f32[512,384]{0,1:T(8,128)S(1)}, u32[]{:S(2)}) copy-start(f32[512,384]{0,1:T(8,128)S(1)} %maximum_bitcast_fusion) | copy-start | bytes 2359300
  77.2 0.7 copy-start.6
  77.2 0.7 copy-start.8
  105.3 4.7 %copy-start.7 = (bf16[512,1,64]{0,2,1:T(8,128)(2,1)S(1)}, bf16[512,1,64]{0,2,1:T(8,128)(2,1)}, u32[]{:S(2)}) copy-start(bf16[512,1,64]{0,2,1:T(8,128)(2,1)} %copy-done.6) | copy-start | bytes 196612
  105.3 4.7 %copy-start.9 = (bf16[512,1,64]{0,2,1:T(8,128)(2,1)S(1)}, bf16[512,1,64]{0,2,1:T(8,128)(2,1)}, u32[]{:S(2)}) copy-start(bf16[512,1,64]{0,2,1:T(8,128)(2,1)} %copy-done.8) | copy-start | bytes 196612
  105.3 30.8 %all-to-all-start.2 = ((bf16[8,64,2048]{2,1,0:T(8,128)(2,1)}), bf16[8,64,2048]{2,1,0:T(8,128)(2,1)S(1)}, u32[]{:S(2)}, u32[]{:S(2)}) async-start(bf16[8,64,2048]{2,1,0:T(8,128)(2,1)} %bitcast.125), calls=%async_computation.2 | async-start | bytes 4194304 | tf_op jit(solution)/shard_map/all_to_all | solution.py:131
  110.1 26.6 %copy-start.3 = (bf16[1,64,2048]{2,1,0:T(8,128)(2,1)S(1)}, bf16[1,64,2048]{2,1,0:T(8,128)(2,1)}, u32[]{:S(2)}) copy-start(bf16[1,64,2048]{2,1,0:T(8,128)(2,1)} %param.14) | copy-start | bytes 786436
  110.1 26.6 %copy-start.10 = (f32[2048]{0:T(1024)S(1)}, f32[2048]{0:T(1024)}, u32[]{:S(2)}) copy-start(f32[2048]{0:T(1024)} %param.21) | copy-start | bytes 24580

commit v3 on v2

v3 whole, which is shorter than its diff:
```python
import functools

import jax
import jax.numpy as jnp
from jax import lax
from jax.sharding import PartitionSpec as P

HEADS = 8
HD = 128
NEW = 512


def rotate(values_in, positions):
    half_dim = values_in.shape[-1] // 2
    exponent = jnp.arange(half_dim, dtype=jnp.float32) * (-2.0 / values_in.shape[-1])
    inverse = jnp.power(jnp.float32(500000.0), exponent)
    angles = positions[:, None] * inverse[None, :]
    cosine = jnp.cos(angles)[:, None, :]
    sine_part = jnp.sin(angles)[:, None, :]
    first_half = values_in[..., :half_dim]
    second_half = values_in[..., half_dim:]
    return jnp.concatenate(
        [
            first_half * cosine - second_half * sine_part,
            second_half * cosine + first_half * sine_part,
        ],
        -1,
    )


def rms_scale(values_in, gain_vector):
    mean_sq = jnp.mean(values_in * values_in, axis=-1, keepdims=True)
    return values_in * lax.rsqrt(mean_sq + 1e-06) * gain_vector


def layer(
    tokens,
    w_q,
    w_k,
    w_v,
    w_o,
    q_gain,
    k_gain,
    out_gain,
    cache_lens,
    group_ids,
    prefix_cache,
    cache_rows,
):
    heads_local = w_q.shape[1] // HD
    width_local = heads_local * HD
    tp_size = lax.axis_size("tp")
    flat_rows = lax.all_to_all(
        jnp.broadcast_to(tokens, (tp_size,) + tokens.shape[1:]), "tp", 0, 0, tiled=True
    ).reshape(-1, tokens.shape[2])
    outgoing = jnp.take(prefix_cache, group_ids, axis=0)
    chosen = lax.all_to_all(outgoing, "req", 0, 0, tiled=True)
    queries = jnp.dot(flat_rows, w_q, preferred_element_type=jnp.float32)
    keys_new = jnp.dot(flat_rows, w_k, preferred_element_type=jnp.float32)
    values_new = jnp.dot(flat_rows, w_v, preferred_element_type=jnp.float32)
    square_sums = lax.psum((jnp.sum(queries * queries, -1), jnp.sum(keys_new * keys_new, -1)), "tp")
    full_width = HEADS * HD
    queries = queries * lax.rsqrt(square_sums[0] / full_width + 1e-06)[:, None] * q_gain
    keys_new = keys_new * lax.rsqrt(square_sums[1] / full_width + 1e-06)[:, None] * k_gain
    prefix_len = prefix_cache.shape[1] * lax.axis_size("req")
    length = cache_lens[0]
    positions = (prefix_len + length + jnp.arange(NEW, dtype=jnp.int32)).astype(jnp.float32)
    q_rot = rotate(queries.reshape(NEW, heads_local, HD), positions).astype(jnp.bfloat16)
    k_rot = rotate(keys_new.reshape(NEW, heads_local, HD), positions).astype(jnp.bfloat16)
    v_new = values_new.reshape(NEW, heads_local, HD).astype(jnp.bfloat16)
    appended = jnp.stack([k_rot, v_new], axis=2).reshape(1, NEW, heads_local * 2 * HD)

    shared = chosen.reshape(-1, heads_local, 2, HD)
    cached = cache_rows[0].reshape(-1, heads_local, 2, HD)
    row_ids = jnp.arange(NEW, dtype=jnp.int32)
    columns = jnp.arange(cached.shape[0], dtype=jnp.int32)
    blocks = (
        (shared[:, :, 0], shared[:, :, 1], None),
        (cached[:, :, 0], cached[:, :, 1], (columns < length)[None, :]),
        (k_rot, v_new, row_ids[None, :] <= row_ids[:, None]),
    )
    scores = []
    for keys_block, _, visible in blocks:
        part = jnp.einsum(
            "qhd,khd->hqk", q_rot, keys_block, preferred_element_type=jnp.float32
        ) * HD ** (-0.5)
        if visible is not None:
            part = jnp.where(visible[None], part, -1e30)
        scores.append(part)
    row_peak = functools.reduce(jnp.maximum, [jnp.max(part, -1) for part in scores])
    denominator = 0.0
    weighted = 0.0
    for (_, values_block, visible), part in zip(blocks, scores):
        weights = jnp.exp(part - row_peak[..., None])
        if visible is not None:
            weights = jnp.where(visible[None], weights, 0.0)
        denominator = denominator + jnp.sum(weights, -1)
        weighted = weighted + jnp.einsum(
            "hqk,khd->hqd",
            weights.astype(jnp.bfloat16),
            values_block,
            preferred_element_type=jnp.float32,
        )
    attended = (
        jnp.transpose(weighted / denominator[..., None], (1, 0, 2))
        .reshape(NEW, width_local)
        .astype(jnp.bfloat16)
    )
    partial_out = jnp.dot(attended, w_o, preferred_element_type=jnp.float32)
    blocks_out = partial_out.astype(jnp.bfloat16).reshape(tp_size, -1, partial_out.shape[1])
    mine = jnp.sum(lax.all_to_all(blocks_out, "tp", 0, 0, tiled=True).astype(jnp.float32), 0)
    hidden = (tokens[0].astype(jnp.float32) + rms_scale(mine, out_gain)).astype(jnp.bfloat16)[None]
    return (hidden, appended)


def solution(mesh):
    return jax.shard_map(
        layer,
        mesh=mesh,
        in_specs=(
            P("req", "tp", None),
            P(None, "tp"),
            P(None, "tp"),
            P(None, "tp"),
            P("tp", None),
            P("tp"),
            P("tp"),
            P(),
            P("req"),
            P(),
            P(None, "req", "tp"),
            P("req", None, "tp"),
        ),
        out_specs=(P("req", "tp", None), P("req", None, "tp")),
        check_vma=False,
    )
```

time: 138 us -> 140 us (1.014)
  the two profiles are of different devices: /device:TPU:1 before, /device:TPU:39 now
where the time goes in v3:
time: 140 us
  waiting for transfers between devices  59 us (42%)
  starting transfers between devices  29 us (21%)
  matrix products  19.3 us (14%)
  blocking collectives  13.3 us (10%)
  local copies, waits for them, and re-layouts  10.1 us (7%)
  other arithmetic  7.38 us (5%)
  between operations  1.55 us (1%)
    all_to_all x1, waiting for transfers between devices, layer(): lax.all_to_all(blocks_out, 'tp', 0, 0, tiled=True).astype(jnp.float32)  30.2 us
    all_to_all x1, waiting for transfers between devices, layer(): lax.all_to_all(jnp.broadcast_to(tokens, (tp_size,) + tokens.shape[1:]), '...  20.5 us
    all_to_all x1, starting transfers between devices, layer(): chosen = lax.all_to_all(outgoing, 'req', 0, 0, tiled=True)  19.6 us
    psum x1, blocking collectives, layer(): lax.psum((jnp.sum(queries * queries, -1), jnp.sum(keys_new * keys_new, -1...  13.3 us
    all_to_all x1, waiting for transfers between devices, layer(): chosen = lax.all_to_all(outgoing, 'req', 0, 0, tiled=True)  8.31 us
    dot_general x3, matrix products, layer(): jnp.einsum('qhd,khd->hqk', q_rot, keys_block, preferred_element_type=jnp....  6.61 us
    dot_general x2, matrix products, layer(): jnp.einsum('hqk,khd->hqd', weights.astype(jnp.bfloat16), values_block, pr...  6.1 us
    unnamed x30, local copies, waits for them, and re-layouts  6.04 us
  transfers between devices with their start and end apart: 3, of which 3 were waited for; matrix products, arithmetic and copies ran while one was open for 13% of the time, Pallas kernels for 0%

profile of v3, /device:TPU:39, one launch (start us, length us, event | category | flops | bytes accessed | tf_op | source)
XLA Modules:
  0.0 139.6 jit_solution(16553629227706530546)
XLA Ops:
  0.6 2.6 %broadcast_in_dim.68 = bf16[8,64,2048]{2,1,0:T(8,128)(2,1)} broadcast(bf16[64,2048]{1,0:T(8,128)(2,1)} %bitcast.64), dimensions={1,2} | broadcast | bytes 2359296 | tf_op jit(solution)/shard_map/broadcast_in_dim | solution.py:54
  3.3 5.2 %all-to-all-start = ((bf16[8,64,2048]{2,1,0:T(8,128)(2,1)}), bf16[8,64,2048]{2,1,0:T(8,128)(2,1)S(1)}, u32[]{:S(2)}, u32[]{:S(2)}) async-start(bf16[8,64,2048]{2,1,0:T(8,128)(2,1)} %broadcast_in_dim.68), calls=%async_computation | async-start | bytes 4194304 | tf_op jit(solution)/shard_map/all_to_all | solution.py:53
  9.2 4.1 %copy.16 = bf16[1,4096,256]{1,2,0:T(8,128)(2,1)} copy(bf16[1,4096,256]{2,1,0:T(8,128)(2,1)} %param.23) | data formatting | bytes 4194304 | tf_op args[11]
  13.3 0.6 gather_fusion
  14.0 0.9 broadcast_select_fusion
  14.9 20.5 %all-to-all-done = bf16[8,64,2048]{2,1,0:T(8,128)(2,1)S(1)} async-done(((bf16[8,64,2048]{2,1,0:T(8,128)(2,1)}), bf16[8,64,2048]{2,1,0:T(8,128)(2,1)S(1)}, u32[]{:S(2)}, u32[]{:S(2)}) %all-to-all-start) | async-done | bytes 2097184 | tf_op jit(solution)/shard_map/all_to_all | solution.py:53
  35.4 19.6 %all-to-all-start.1 = ((bf16[64,16,256]{2,1,0:T(8,128)(2,1)}), bf16[64,16,256]{2,1,0:T(8,128)(2,1)S(1)}, u32[]{:S(2)}, u32[]{:S(2)}) async-start(bf16[64,16,256]{2,1,0:T(8,128)(2,1)} %broadcast_select_fusion), calls=%async_computation.1 | async-start | bytes 1048576 | tf_op jit(solution)/shard_map/all_to_all | solution.py:57
  55.0 2.6 %multiply_reduce_fusion.2 = (f32[512]{0:T(512)S(1)}, f32[512,128]{0,1:T(8,128)}) fusion(bf16[512,2048]{1,0:T(8,128)(2,1)S(1)} %bitcast.57, bf16[2048,128]{1,0:T(8,128)(2,1)} %param.14), kind=kOutput, calls=%fused_computation.45 | convolution fusion | flops 268566016 | bytes 2885632 | tf_op jit(solution)/shard_map/dot_general | solution.py:59
  57.7 0.9 multiply_reduce_fusion.3
  58.5 13.3 %all-reduce = (f32[512]{0:T(512)S(1)}, f32[512]{0:T(512)S(1)}) all-reduce(f32[512]{0:T(512)S(1)} %get-tuple-element.18, f32[512]{0:T(512)S(1)} %get-tuple-element.20), channel_id=1, replica_groups=mesh['req'=64,'tp'=8] {'tp'}, use_global_device_ids=true, to_apply=%region_1.2 | all-reduce | flops 1024 | bytes 8192 | tf_op jit(solution)/shard_map/psum | solution.py:61
  71.8 1.1 multiply_bitcast_fusion
  73.7 1.3 fusion.63
  75.0 0.8 convolution_convert_fusion.1
  75.8 4.7 %fusion = (f32[512]{0:T(512)S(1)}, f32[512,4096]{1,0:T(8,128)}) fusion(pred[4096]{0:T(1024)(128)(4,1)S(1)} %iota_compare_fusion.1, bf16[4096,1,2,128]{0,3,2,1:T(8,128)(2,1)S(1)} %bitcast.61, bf16[512,64]{0,1:T(8,128)(2,1)S(1)} %get-tuple-element.16, bf16[512,64]{0,1:T(8,128)(2,1)S(1)} %get-tuple-element.17), kind=kOutput, calls=%fused_computation.3 | convolution fusion | flops 543424000 | bytes 9574400 | tf_op jit(solution)/shard_map/qhd,khd->hqk/dot_general | solution.py:84
  80.6 8.3 %all-to-all-done.1 = bf16[64,16,256]{2,1,0:T(8,128)(2,1)S(1)} async-done(((bf16[64,16,256]{2,1,0:T(8,128)(2,1)}), bf16[64,16,256]{2,1,0:T(8,128)(2,1)S(1)}, u32[]{:S(2)}, u32[]{:S(2)}) %all-to-all-start.1) | async-done | bytes 524320 | tf_op jit(solution)/shard_map/all_to_all | solution.py:57
  89.0 0.7 fusion.62
  90.6 5.6 %fusion.3 = f32[512,128]{1,0:T(8,128)S(1)} fusion(f32[512,4096]{1,0:T(8,128)} %get-tuple-element.27, f32[512]{0:T(512)S(1)} %maximum_maximum_fusion, pred[4096]{0:T(1024)(128)(4,1)S(1)} %iota_compare_fusion.1, bf16[4096,1,2,128]{0,3,2,1:T(8,128)(2,1)S(1)} %bitcast.62), kind=kOutput, calls=%fused_computation.7 | convolution fusion | flops 547356672 | bytes 9705472 | tf_op jit(solution)/shard_map/hqk,khd->hqd/dot_general | solution.py:98
  96.2 2.6 %fusion.1 = f32[512]{0:T(512)S(1)} fusion(f32[512,4096]{1,0:T(8,128)S(1)} %bitcast.56, f32[512]{0:T(512)S(1)} %maximum_maximum_fusion, pred[4096]{0:T(1024)(128)(4,1)S(1)} %iota_compare_fusion.1), kind=kLoop, calls=%fused_computation.4 | loop fusion | flops 10485248 | bytes 8396800 | tf_op jit(solution)/shard_map/reduce_sum | solution.py:97
  99.3 0.7 copy-done.3
  100.7 2.2 %convolution_convert_fusion = bf16[512,2048]{1,0:T(8,128)(2,1)} fusion(bf16[128,2048]{1,0:T(8,128)(2,1)S(1)} %copy-done, f32[512,128]{1,0:T(8,128)S(1)} %convolution_add_fusion.1, bf16[512,128]{0,1:T(8,128)(2,1)S(1)} %convolution_convert_fusion.1, f32[512,512]{0,1:T(8,128)S(1)} %copy-done.3, f32[512]{0:T(512)S(1)} %maximum_maximum_fusion, ...), kind=kOutput, calls=%fused_computation.9 | convolution fusion | flops 337838080 | bytes 4067328 | tf_op jit(solution)/shard_map/dot_general | solution.py:109
  103.0 4.2 %all-to-all-start.2 = ((bf16[8,64,2048]{2,1,0:T(8,128)(2,1)}), bf16[8,64,2048]{2,1,0:T(8,128)(2,1)S(1)}, u32[]{:S(2)}, u32[]{:S(2)}) async-start(bf16[8,64,2048]{2,1,0:T(8,128)(2,1)} %bitcast.60), calls=%async_computation.2 | async-start | bytes 4194304 | tf_op jit(solution)/shard_map/all_to_all | solution.py:111
  107.2 0.8 copy.19
  108.1 30.2 %all-to-all-done.2 = bf16[8,64,2048]{2,1,0:T(8,128)(2,1)S(1)} async-done(((bf16[8,64,2048]{2,1,0:T(8,128)(2,1)}), bf16[8,64,2048]{2,1,0:T(8,128)(2,1)S(1)}, u32[]{:S(2)}, u32[]{:S(2)}) %all-to-all-start.2) | async-done | bytes 2097184 | tf_op jit(solution)/shard_map/all_to_all | solution.py:111
  138.8 0.9 fusion.21
  (48 shorter events, 3.5 us)
Async XLA Ops:
  0.6 100.1 %copy-start = (bf16[128,2048]{1,0:T(8,128)(2,1)S(1)}, bf16[128,2048]{1,0:T(8,128)(2,1)}, u32[]{:S(2)}) copy-start(bf16[128,2048]{1,0:T(8,128)(2,1)} %param.16) | copy-start | bytes 1572868
  3.3 32.2 %all-to-all-start = ((bf16[8,64,2048]{2,1,0:T(8,128)(2,1)}), bf16[8,64,2048]{2,1,0:T(8,128)(2,1)S(1)}, u32[]{:S(2)}, u32[]{:S(2)}) async-start(bf16[8,64,2048]{2,1,0:T(8,128)(2,1)} %broadcast_in_dim.68), calls=%async_computation | async-start | bytes 4194304 | tf_op jit(solution)/shard_map/all_to_all | solution.py:53
  9.1 4.2 %copy-start.11 = (s32[64]{0:T(128)S(1)}, s32[64]{0:T(128)}, u32[]{:S(2)}) copy-start(s32[64]{0:T(128)} %param.21) | copy-start | bytes 772
  9.1 4.2 %copy-start.4 = (bf16[8,16,256]{2,1,0:T(8,128)(2,1)S(1)}, bf16[8,16,256]{2,1,0:T(8,128)(2,1)}, u32[]{:S(2)}) copy-start(bf16[8,16,256]{2,1,0:T(8,128)(2,1)} %param.22) | copy-start | bytes 196612
  35.4 53.4 %all-to-all-start.1 = ((bf16[64,16,256]{2,1,0:T(8,128)(2,1)}), bf16[64,16,256]{2,1,0:T(8,128)(2,1)S(1)}, u32[]{:S(2)}, u32[]{:S(2)}) async-start(bf16[64,16,256]{2,1,0:T(8,128)(2,1)} %broadcast_select_fusion), calls=%async_computation.1 | async-start | bytes 1048576 | tf_op jit(solution)/shard_map/all_to_all | solution.py:57
  55.0 2.6 %copy-start.6 = (bf16[2048,128]{1,0:T(8,128)(2,1)S(1)}, bf16[2048,128]{1,0:T(8,128)(2,1)}, u32[]{:S(2)}) copy-start(bf16[2048,128]{1,0:T(8,128)(2,1)} %param.13) | copy-start | bytes 1572868
  57.7 14.2 %copy-start.9 = (f32[128]{0:T(128)S(1)}, f32[128]{0:T(128)}, u32[]{:S(2)}) copy-start(f32[128]{0:T(128)} %param.18) | copy-start | bytes 1540
  57.7 15.3 %copy-start.10 = (f32[128]{0:T(128)S(1)}, f32[128]{0:T(128)}, u32[]{:S(2)}) copy-start(f32[128]{0:T(128)} %param.17) | copy-start | bytes 1540
  71.8 3.2 %copy-start.7 = (bf16[2048,128]{1,0:T(8,128)(2,1)S(1)}, bf16[2048,128]{1,0:T(8,128)(2,1)}, u32[]{:S(2)}) copy-start(bf16[2048,128]{1,0:T(8,128)(2,1)} %param.15) | copy-start | bytes 1572868
  73.6 2.2 %copy-start.1 = (bf16[1,4096,256]{1,2,0:T(8,128)(2,1)S(1)}, bf16[1,4096,256]{1,2,0:T(8,128)(2,1)}, u32[]{:S(2)}) copy-start(bf16[1,4096,256]{1,2,0:T(8,128)(2,1)} %copy.16) | copy-start | bytes 6291460
  89.0 1.6 %copy-start.2 = (bf16[1,4096,256]{1,2,0:T(8,128)(2,1)S(1)}, bf16[1,4096,256]{1,2,0:T(8,128)(2,1)}, u32[]{:S(2)}) copy-start(bf16[1,4096,256]{1,2,0:T(8,128)(2,1)} %copy.16) | copy-start | bytes 6291460
  89.8 6.4 %slice-start = ((s8[8388608]{0:T(1024)(128)(4,1)}), s8[4194304]{0:T(1024)(128)(4,1)S(1)}, s32[]{:S(2)}) async-start(s8[8388608]{0:T(1024)(128)(4,1)} %bitcast.55), calls=%async_computation.3 | async-start | bytes 8388608
  90.6 5.6 %slice-start.1 = ((s8[8388608]{0:T(1024)(128)(4,1)}), s8[4194304]{0:T(1024)(128)(4,1)S(1)}, s32[]{:S(2)}) async-start(s8[8388608]{0:T(1024)(128)(4,1)} %bitcast.55), calls=%async_computation.4 | async-start | bytes 8388608
  98.8 1.2 copy-start.3
  103.0 35.3 %all-to-all-start.2 = ((bf16[8,64,2048]{2,1,0:T(8,128)(2,1)}), bf16[8,64,2048]{2,1,0:T(8,128)(2,1)S(1)}, u32[]{:S(2)}, u32[]{:S(2)}) async-start(bf16[8,64,2048]{2,1,0:T(8,128)(2,1)} %bitcast.60), calls=%async_computation.2 | async-start | bytes 4194304 | tf_op jit(solution)/shard_map/all_to_all | solution.py:111
  107.2 31.6 %copy-start.5 = (bf16[1,64,2048]{2,1,0:T(8,128)(2,1)S(1)}, bf16[1,64,2048]{2,1,0:T(8,128)(2,1)}, u32[]{:S(2)}) copy-start(bf16[1,64,2048]{2,1,0:T(8,128)(2,1)} %param.12) | copy-start | bytes 786436
  107.2 31.6 %copy-start.8 = (f32[2048]{0:T(1024)S(1)}, f32[2048]{0:T(1024)}, u32[]{:S(2)}) copy-start(f32[2048]{0:T(1024)} %param.19) | copy-start | bytes 24580

commit v4 on v3

--- a/solution.py
+++ b/solution.py
@@ -33,6 +33,17 @@
     return values_in * lax.rsqrt(mean_sq + 1e-06) * gain_vector
 
 
+def exchange_sum(own, axis, size):
+    index = lax.axis_index(axis)
+    parts = [own]
+    for shift in range(1, size):
+        parts.append(lax.ppermute(own, axis, [(i, (i + shift) % size) for i in range(size)]))
+    stacked = jnp.stack(parts)
+    order = (index - jnp.arange(size)) % size
+    by_source = jnp.zeros_like(stacked).at[order].set(stacked)
+    return functools.reduce(lambda a, b: a + b, [by_source[i] for i in range(size)])
+
+
 def layer(
     tokens,
     w_q,
@@ -58,7 +69,8 @@
     queries = jnp.dot(flat_rows, w_q, preferred_element_type=jnp.float32)
     keys_new = jnp.dot(flat_rows, w_k, preferred_element_type=jnp.float32)
     values_new = jnp.dot(flat_rows, w_v, preferred_element_type=jnp.float32)
-    square_sums = lax.psum((jnp.sum(queries * queries, -1), jnp.sum(keys_new * keys_new, -1)), "tp")
+    own_sums = jnp.stack([jnp.sum(queries * queries, -1), jnp.sum(keys_new * keys_new, -1)])
+    square_sums = exchange_sum(own_sums, "tp", tp_size)
     full_width = HEADS * HD
     queries = queries * lax.rsqrt(square_sums[0] / full_width + 1e-06)[:, None] * q_gain
     keys_new = keys_new * lax.rsqrt(square_sums[1] / full_width + 1e-06)[:, None] * k_gain

time: 140 us -> 146 us (1.043)
  the two profiles are of different devices: /device:TPU:39 before, /device:TPU:1 now
where the time goes in v4:
time: 146 us; the launch traced here: 145 us
  waiting for transfers between devices  55.9 us (38%)
  starting transfers between devices  50 us (34%)
  matrix products  19.5 us (13%)
  local copies, waits for them, and re-layouts  11.6 us (8%)
  other arithmetic  6.35 us (4%)
  between operations  1.73 us (1%)
    all_to_all x1, waiting for transfers between devices, layer(): lax.all_to_all(blocks_out, 'tp', 0, 0, tiled=True).astype(jnp.float32)  26.1 us
    ppermute x7, starting transfers between devices, exchange_sum(): lax.ppermute(own, axis, [(i, (i + shift) % size) for i in range(size)])  21.5 us
    all_to_all x1, waiting for transfers between devices, layer(): lax.all_to_all(jnp.broadcast_to(tokens, (tp_size,) + tokens.shape[1:]), '...  20.7 us
    all_to_all x1, starting transfers between devices, layer(): chosen = lax.all_to_all(outgoing, 'req', 0, 0, tiled=True)  19 us
    ppermute x7, waiting for transfers between devices, exchange_sum(): lax.ppermute(own, axis, [(i, (i + shift) % size) for i in range(size)])  9.09 us
    dot_general x3, matrix products, layer(): jnp.einsum('qhd,khd->hqk', q_rot, keys_block, preferred_element_type=jnp....  6.67 us
    dot_general x2, matrix products, layer(): jnp.einsum('hqk,khd->hqd', weights.astype(jnp.bfloat16), values_block, pr...  5.98 us
    all_to_all x1, starting transfers between devices, layer(): lax.all_to_all(jnp.broadcast_to(tokens, (tp_size,) + tokens.shape[1:]), '...  5.85 us
  transfers between devices with their start and end apart: 10, of which 5 were waited for; matrix products, arithmetic and copies ran while one was open for 13% of the time, Pallas kernels for 0%

profile of v4, /device:TPU:1, one launch (start us, length us, event | category | flops | bytes accessed | tf_op | source)
XLA Modules:
  0.0 145.1 jit_solution(11659797457664724436)
XLA Ops:
  0.6 2.6 %broadcast_in_dim.72 = bf16[8,64,2048]{2,1,0:T(8,128)(2,1)} broadcast(bf16[64,2048]{1,0:T(8,128)(2,1)} %bitcast.87), dimensions={1,2} | broadcast | bytes 2359296 | tf_op jit(solution)/shard_map/broadcast_in_dim | solution.py:65
  3.2 5.9 %all-to-all-start = ((bf16[8,64,2048]{2,1,0:T(8,128)(2,1)}), bf16[8,64,2048]{2,1,0:T(8,128)(2,1)S(1)}, u32[]{:S(2)}, u32[]{:S(2)}) async-start(bf16[8,64,2048]{2,1,0:T(8,128)(2,1)} %broadcast_in_dim.72), calls=%async_computation | async-start | bytes 4194304 | tf_op jit(solution)/shard_map/all_to_all | solution.py:64
  9.7 4.1 %copy.16 = bf16[1,4096,256]{1,2,0:T(8,128)(2,1)} copy(bf16[1,4096,256]{2,1,0:T(8,128)(2,1)} %param.23) | data formatting | bytes 4194304 | tf_op args[11]
  15.5 20.7 %all-to-all-done = bf16[8,64,2048]{2,1,0:T(8,128)(2,1)S(1)} async-done(((bf16[8,64,2048]{2,1,0:T(8,128)(2,1)}), bf16[8,64,2048]{2,1,0:T(8,128)(2,1)S(1)}, u32[]{:S(2)}, u32[]{:S(2)}) %all-to-all-start) | async-done | bytes 2097184 | tf_op jit(solution)/shard_map/all_to_all | solution.py:64
  36.2 19.0 %all-to-all-start.1 = ((bf16[64,16,256]{2,1,0:T(8,128)(2,1)}), bf16[64,16,256]{2,1,0:T(8,128)(2,1)}, u32[]{:S(2)}, u32[]{:S(2)}) async-start(bf16[64,16,256]{2,1,0:T(8,128)(2,1)} %broadcast_select_fusion), calls=%async_computation.1 | async-start | bytes 1048576 | tf_op jit(solution)/shard_map/all_to_all | solution.py:68
  55.1 1.9 %multiply_reduce_fusion.3 = (f32[512]{0:T(512)S(1)}, f32[512,128]{0,1:T(8,128)S(1)}) fusion(bf16[512,2048]{1,0:T(8,128)(2,1)S(1)} %bitcast.80, bf16[2048,128]{1,0:T(8,128)(2,1)} %param.13), kind=kOutput, calls=%fused_computation.48 | convolution fusion | flops 268566016 | bytes 2885632 | tf_op jit(solution)/shard_map/dot_general | solution.py:69
  57.0 1.9 %multiply_reduce_fusion.2 = (f32[512]{0:T(512)S(1)}, f32[512,128]{0,1:T(8,128)S(1)}) fusion(bf16[512,2048]{1,0:T(8,128)(2,1)S(1)} %bitcast.81, bf16[2048,128]{1,0:T(8,128)(2,1)} %param.14), kind=kOutput, calls=%fused_computation.47 | convolution fusion | flops 268566016 | bytes 2885632 | tf_op jit(solution)/shard_map/dot_general | solution.py:70
  59.0 2.6 %collective-permute-start.5 = (f32[2,512]{1,0:T(2,128)S(1)}, f32[2,512]{1,0:T(2,128)S(1)}, u32[]{:S(2)}, u32[]{:S(2)}) collective-permute-start(f32[2,512]{1,0:T(2,128)S(1)} %pad_maximum_fusion.5), channel_id=1, source_target_pairs={{0,6},{1,7},{2,0},{3,1},{4,2},{5,3},{6,4},{7,5},{8,14},{9,15},{10,... | collective-permute-start | bytes 12296 | tf_op jit(solution)/shard_map/ppermute | solution.py:40
  61.6 6.3 %collective-permute-start.4 = (f32[2,512]{1,0:T(2,128)S(1)}, f32[2,512]{1,0:T(2,128)S(1)}, u32[]{:S(2)}, u32[]{:S(2)}) collective-permute-start(f32[2,512]{1,0:T(2,128)S(1)} %pad_maximum_fusion.5), channel_id=1, source_target_pairs={{0,5},{1,6},{2,7},{3,0},{4,1},{5,2},{6,3},{7,4},{8,13},{9,14},{10,... | collective-permute-start | bytes 12296 | tf_op jit(solution)/shard_map/ppermute | solution.py:40
  67.9 2.5 %collective-permute-start.3 = (f32[2,512]{1,0:T(2,128)S(1)}, f32[2,512]{1,0:T(2,128)S(1)}, u32[]{:S(2)}, u32[]{:S(2)}) collective-permute-start(f32[2,512]{1,0:T(2,128)S(1)} %pad_maximum_fusion.5), channel_id=1, source_target_pairs={{0,4},{1,5},{2,6},{3,7},{4,0},{5,1},{6,2},{7,3},{8,12},{9,13},{10,... | collective-permute-start | bytes 12296 | tf_op jit(solution)/shard_map/ppermute | solution.py:40
  70.4 1.9 %collective-permute-start.2 = (f32[2,512]{1,0:T(2,128)S(1)}, f32[2,512]{1,0:T(2,128)S(1)}, u32[]{:S(2)}, u32[]{:S(2)}) collective-permute-start(f32[2,512]{1,0:T(2,128)S(1)} %pad_maximum_fusion.5), channel_id=1, source_target_pairs={{0,3},{1,4},{2,5},{3,6},{4,7},{5,0},{6,1},{7,2},{8,11},{9,12},{10,... | collective-permute-start | bytes 12296 | tf_op jit(solution)/shard_map/ppermute | solution.py:40
  72.3 4.0 %collective-permute-start = (f32[2,512]{1,0:T(2,128)S(1)}, f32[2,512]{1,0:T(2,128)S(1)}, u32[]{:S(2)}, u32[]{:S(2)}) collective-permute-start(f32[2,512]{1,0:T(2,128)S(1)} %pad_maximum_fusion.5), channel_id=1, source_target_pairs={{0,1},{1,2},{2,3},{3,4},{4,5},{5,6},{6,7},{7,0},{8,9},{9,10},{10,1... | collective-permute-start | bytes 12296 | tf_op jit(solution)/shard_map/ppermute | solution.py:40
  77.2 2.0 %collective-permute-done = f32[2,512]{1,0:T(2,128)S(1)} collective-permute-done((f32[2,512]{1,0:T(2,128)S(1)}, f32[2,512]{1,0:T(2,128)S(1)}, u32[]{:S(2)}, u32[]{:S(2)}) %collective-permute-start) | collective-permute-done | bytes 4128 | tf_op jit(solution)/shard_map/ppermute | solution.py:40
  79.2 2.2 %collective-permute-start.1 = (f32[2,512]{1,0:T(2,128)S(1)}, f32[2,512]{1,0:T(2,128)S(1)}, u32[]{:S(2)}, u32[]{:S(2)}) collective-permute-start(f32[2,512]{1,0:T(2,128)S(1)} %pad_maximum_fusion.5), channel_id=1, source_target_pairs={{0,2},{1,3},{2,4},{3,5},{4,6},{5,7},{6,0},{7,1},{8,10},{9,11},{10,... | collective-permute-start | bytes 12296 | tf_op jit(solution)/shard_map/ppermute | solution.py:40
  81.4 4.9 %collective-permute-done.1 = f32[2,512]{1,0:T(2,128)S(1)} collective-permute-done((f32[2,512]{1,0:T(2,128)S(1)}, f32[2,512]{1,0:T(2,128)S(1)}, u32[]{:S(2)}, u32[]{:S(2)}) %collective-permute-start.1) | collective-permute-done | bytes 4128 | tf_op jit(solution)/shard_map/ppermute | solution.py:40
  86.4 2.1 %collective-permute-start.6 = (f32[2,512]{1,0:T(2,128)S(1)}, f32[2,512]{1,0:T(2,128)S(1)}, u32[]{:S(2)}, u32[]{:S(2)}) collective-permute-start(f32[2,512]{1,0:T(2,128)S(1)} %pad_maximum_fusion.5), channel_id=1, source_target_pairs={{0,7},{1,0},{2,1},{3,2},{4,3},{5,4},{6,5},{7,6},{8,15},{9,8},{10,9... | collective-permute-start | bytes 12296 | tf_op jit(solution)/shard_map/ppermute | solution.py:40
  88.6 2.1 %collective-permute-done.6 = f32[2,512]{1,0:T(2,128)S(1)} collective-permute-done((f32[2,512]{1,0:T(2,128)S(1)}, f32[2,512]{1,0:T(2,128)S(1)}, u32[]{:S(2)}, u32[]{:S(2)}) %collective-permute-start.6) | collective-permute-done | bytes 4128 | tf_op jit(solution)/shard_map/ppermute | solution.py:40
  92.2 1.4 fusion.69
  93.6 4.7 %fusion = (f32[512]{0:T(512)S(1)}, f32[512,4096]{1,0:T(8,128)}) fusion(pred[4096]{0:T(1024)(128)(4,1)S(1)} %iota_compare_fusion.1, bf16[4096,1,2,128]{0,3,2,1:T(8,128)(2,1)S(1)} %bitcast.84, bf16[512,64]{0,1:T(8,128)(2,1)S(1)} %get-tuple-element.16, bf16[512,64]{0,1:T(8,128)(2,1)S(1)} %get-tuple-element.17), kind=kOutput, calls=%fused_computation.4 | convolution fusion | flops 543424000 | bytes 9574400 | tf_op jit(solution)/shard_map/qhd,khd->hqk/dot_general | solution.py:96
  100.8 5.4 %fusion.3 = f32[512,128]{1,0:T(8,128)S(1)} fusion(f32[512,4096]{1,0:T(8,128)} %get-tuple-element.27, f32[512]{0:T(512)S(1)} %maximum_maximum_fusion, pred[4096]{0:T(1024)(128)(4,1)S(1)} %iota_compare_fusion.1, bf16[4096,1,2,128]{0,3,2,1:T(8,128)(2,1)S(1)} %bitcast.85), kind=kOutput, calls=%fused_computation.8 | convolution fusion | flops 547356672 | bytes 9705472 | tf_op jit(solution)/shard_map/hqk,khd->hqd/dot_general | solution.py:110
  106.3 2.6 %fusion.1 = f32[512]{0:T(512)S(1)} fusion(f32[512,4096]{1,0:T(8,128)S(1)} %bitcast.79, f32[512]{0:T(512)S(1)} %maximum_maximum_fusion, pred[4096]{0:T(1024)(128)(4,1)S(1)} %iota_compare_fusion.1), kind=kLoop, calls=%fused_computation.5 | loop fusion | flops 10485248 | bytes 8396800 | tf_op jit(solution)/shard_map/reduce_sum | solution.py:109
  110.8 2.2 %convolution_convert_fusion = bf16[512,2048]{1,0:T(8,128)(2,1)} fusion(bf16[128,2048]{1,0:T(8,128)(2,1)S(1)} %copy-done, f32[512,128]{1,0:T(8,128)S(1)} %convolution_add_fusion.1, bf16[512,128]{0,1:T(8,128)(2,1)S(1)} %convolution_convert_fusion.1, f32[512,512]{0,1:T(8,128)S(1)} %copy-done.2, f32[512]{0:T(512)S(1)} %maximum_maximum_fusion, ...), kind=kOutput, calls=%fused_computation.10 | convolution fusion | flops 337838080 | bytes 4067328 | tf_op jit(solution)/shard_map/dot_general | solution.py:121
  113.0 3.6 %all-to-all-start.2 = ((bf16[8,64,2048]{2,1,0:T(8,128)(2,1)}), bf16[8,64,2048]{2,1,0:T(8,128)(2,1)S(1)}, u32[]{:S(2)}, u32[]{:S(2)}) async-start(bf16[8,64,2048]{2,1,0:T(8,128)(2,1)} %bitcast.83), calls=%async_computation.2 | async-start | bytes 4194304 | tf_op jit(solution)/shard_map/all_to_all | solution.py:123
  117.5 26.1 %all-to-all-done.2 = bf16[8,64,2048]{2,1,0:T(8,128)(2,1)S(1)} async-done(((bf16[8,64,2048]{2,1,0:T(8,128)(2,1)}), bf16[8,64,2048]{2,1,0:T(8,128)(2,1)S(1)}, u32[]{:S(2)}, u32[]{:S(2)}) %all-to-all-start.2) | async-done | bytes 2097184 | tf_op jit(solution)/shard_map/all_to_all | solution.py:123
  (69 shorter events, 10.6 us)
Async XLA Ops:
  0.6 110.2 %copy-start = (bf16[128,2048]{1,0:T(8,128)(2,1)S(1)}, bf16[128,2048]{1,0:T(8,128)(2,1)}, u32[]{:S(2)}) copy-start(bf16[128,2048]{1,0:T(8,128)(2,1)} %param.16) | copy-start | bytes 1572868
  3.2 33.0 %all-to-all-start = ((bf16[8,64,2048]{2,1,0:T(8,128)(2,1)}), bf16[8,64,2048]{2,1,0:T(8,128)(2,1)S(1)}, u32[]{:S(2)}, u32[]{:S(2)}) async-start(bf16[8,64,2048]{2,1,0:T(8,128)(2,1)} %broadcast_in_dim.72), calls=%async_computation | async-start | bytes 4194304 | tf_op jit(solution)/shard_map/all_to_all | solution.py:64
  9.7 4.2 %copy-start.9 = (s32[64]{0:T(128)S(1)}, s32[64]{0:T(128)}, u32[]{:S(2)}) copy-start(s32[64]{0:T(128)} %param.21) | copy-start | bytes 772
  9.7 4.2 %copy-start.3 = (bf16[8,16,256]{2,1,0:T(8,128)(2,1)S(1)}, bf16[8,16,256]{2,1,0:T(8,128)(2,1)}, u32[]{:S(2)}) copy-start(bf16[8,16,256]{2,1,0:T(8,128)(2,1)} %param.22) | copy-start | bytes 196612
  36.2 62.2 %all-to-all-start.1 = ((bf16[64,16,256]{2,1,0:T(8,128)(2,1)}), bf16[64,16,256]{2,1,0:T(8,128)(2,1)}, u32[]{:S(2)}, u32[]{:S(2)}) async-start(bf16[64,16,256]{2,1,0:T(8,128)(2,1)} %broadcast_select_fusion), calls=%async_computation.1 | async-start | bytes 1048576 | tf_op jit(solution)/shard_map/all_to_all | solution.py:68
  57.0 19.3 %copy-start.5 = (bf16[2048,128]{1,0:T(8,128)(2,1)S(1)}, bf16[2048,128]{1,0:T(8,128)(2,1)}, u32[]{:S(2)}) copy-start(bf16[2048,128]{1,0:T(8,128)(2,1)} %param.15) | copy-start | bytes 1572868
  59.0 32.5 %copy-start.7 = (f32[128]{0:T(128)S(1)}, f32[128]{0:T(128)}, u32[]{:S(2)}) copy-start(f32[128]{0:T(128)} %param.18) | copy-start | bytes 1540
  59.0 32.5 %copy-start.8 = (f32[128]{0:T(128)S(1)}, f32[128]{0:T(128)}, u32[]{:S(2)}) copy-start(f32[128]{0:T(128)} %param.17) | copy-start | bytes 1540
  59.0 29.5 %collective-permute-start.5 = (f32[2,512]{1,0:T(2,128)S(1)}, f32[2,512]{1,0:T(2,128)S(1)}, u32[]{:S(2)}, u32[]{:S(2)}) collective-permute-start(f32[2,512]{1,0:T(2,128)S(1)} %pad_maximum_fusion.5), channel_id=1, source_target_pairs={{0,6},{1,7},{2,0},{3,1},{4,2},{5,3},{6,4},{7,5},{8,14},{9,15},{10,... | collective-permute-start | bytes 12296 | tf_op jit(solution)/shard_map/ppermute | solution.py:40
  61.6 26.9 %collective-permute-start.4 = (f32[2,512]{1,0:T(2,128)S(1)}, f32[2,512]{1,0:T(2,128)S(1)}, u32[]{:S(2)}, u32[]{:S(2)}) collective-permute-start(f32[2,512]{1,0:T(2,128)S(1)} %pad_maximum_fusion.5), channel_id=1, source_target_pairs={{0,5},{1,6},{2,7},{3,0},{4,1},{5,2},{6,3},{7,4},{8,13},{9,14},{10,... | collective-permute-start | bytes 12296 | tf_op jit(solution)/shard_map/ppermute | solution.py:40
  67.9 20.6 %collective-permute-start.3 = (f32[2,512]{1,0:T(2,128)S(1)}, f32[2,512]{1,0:T(2,128)S(1)}, u32[]{:S(2)}, u32[]{:S(2)}) collective-permute-start(f32[2,512]{1,0:T(2,128)S(1)} %pad_maximum_fusion.5), channel_id=1, source_target_pairs={{0,4},{1,5},{2,6},{3,7},{4,0},{5,1},{6,2},{7,3},{8,12},{9,13},{10,... | collective-permute-start | bytes 12296 | tf_op jit(solution)/shard_map/ppermute | solution.py:40
  70.4 18.0 %collective-permute-start.2 = (f32[2,512]{1,0:T(2,128)S(1)}, f32[2,512]{1,0:T(2,128)S(1)}, u32[]{:S(2)}, u32[]{:S(2)}) collective-permute-start(f32[2,512]{1,0:T(2,128)S(1)} %pad_maximum_fusion.5), channel_id=1, source_target_pairs={{0,3},{1,4},{2,5},{3,6},{4,7},{5,0},{6,1},{7,2},{8,11},{9,12},{10,... | collective-permute-start | bytes 12296 | tf_op jit(solution)/shard_map/ppermute | solution.py:40
  72.3 6.9 %collective-permute-start = (f32[2,512]{1,0:T(2,128)S(1)}, f32[2,512]{1,0:T(2,128)S(1)}, u32[]{:S(2)}, u32[]{:S(2)}) collective-permute-start(f32[2,512]{1,0:T(2,128)S(1)} %pad_maximum_fusion.5), channel_id=1, source_target_pairs={{0,1},{1,2},{2,3},{3,4},{4,5},{5,6},{6,7},{7,0},{8,9},{9,10},{10,1... | collective-permute-start | bytes 12296 | tf_op jit(solution)/shard_map/ppermute | solution.py:40
  77.2 16.4 %copy-start.1 = (bf16[1,4096,256]{1,2,0:T(8,128)(2,1)S(1)}, bf16[1,4096,256]{1,2,0:T(8,128)(2,1)}, u32[]{:S(2)}) copy-start(bf16[1,4096,256]{1,2,0:T(8,128)(2,1)} %copy.16) | copy-start | bytes 6291460
  79.2 7.1 %collective-permute-start.1 = (f32[2,512]{1,0:T(2,128)S(1)}, f32[2,512]{1,0:T(2,128)S(1)}, u32[]{:S(2)}, u32[]{:S(2)}) collective-permute-start(f32[2,512]{1,0:T(2,128)S(1)} %pad_maximum_fusion.5), channel_id=1, source_target_pairs={{0,2},{1,3},{2,4},{3,5},{4,6},{5,7},{6,0},{7,1},{8,10},{9,11},{10,... | collective-permute-start | bytes 12296 | tf_op jit(solution)/shard_map/ppermute | solution.py:40
  86.4 4.3 %collective-permute-start.6 = (f32[2,512]{1,0:T(2,128)S(1)}, f32[2,512]{1,0:T(2,128)S(1)}, u32[]{:S(2)}, u32[]{:S(2)}) collective-permute-start(f32[2,512]{1,0:T(2,128)S(1)} %pad_maximum_fusion.5), channel_id=1, source_target_pairs={{0,7},{1,0},{2,1},{3,2},{4,3},{5,4},{6,5},{7,6},{8,15},{9,8},{10,9... | collective-permute-start | bytes 12296 | tf_op jit(solution)/shard_map/ppermute | solution.py:40
  100.3 6.0 %slice-start = ((s8[8388608]{0:T(1024)(128)(4,1)}), s8[4194304]{0:T(1024)(128)(4,1)S(1)}, s32[]{:S(2)}) async-start(s8[8388608]{0:T(1024)(128)(4,1)} %bitcast.78), calls=%async_computation.3 | async-start | bytes 8388608
  100.8 5.5 %slice-start.1 = ((s8[8388608]{0:T(1024)(128)(4,1)}), s8[4194304]{0:T(1024)(128)(4,1)S(1)}, s32[]{:S(2)}) async-start(s8[8388608]{0:T(1024)(128)(4,1)} %bitcast.78), calls=%async_computation.4 | async-start | bytes 8388608
  108.9 1.2 copy-start.2
  113.0 30.7 %all-to-all-start.2 = ((bf16[8,64,2048]{2,1,0:T(8,128)(2,1)}), bf16[8,64,2048]{2,1,0:T(8,128)(2,1)S(1)}, u32[]{:S(2)}, u32[]{:S(2)}) async-start(bf16[8,64,2048]{2,1,0:T(8,128)(2,1)} %bitcast.83), calls=%async_computation.2 | async-start | bytes 4194304 | tf_op jit(solution)/shard_map/all_to_all | solution.py:123
  116.6 27.6 %copy-start.4 = (bf16[1,64,2048]{2,1,0:T(8,128)(2,1)S(1)}, bf16[1,64,2048]{2,1,0:T(8,128)(2,1)}, u32[]{:S(2)}) copy-start(bf16[1,64,2048]{2,1,0:T(8,128)(2,1)} %param.12) | copy-start | bytes 786436
  116.7 27.5 %copy-start.6 = (f32[2048]{0:T(1024)S(1)}, f32[2048]{0:T(1024)}, u32[]{:S(2)}) copy-start(f32[2048]{0:T(1024)} %param.19) | copy-start | bytes 24580

commit v5 on v3

--- a/solution.py
+++ b/solution.py
@@ -1,8 +1,8 @@
-import functools
-
 import jax
 import jax.numpy as jnp
 from jax import lax
+from jax.experimental import pallas as pl
+from jax.experimental.pallas import tpu as pltpu
 from jax.sharding import PartitionSpec as P
 
 HEADS = 8
@@ -33,6 +33,95 @@
     return values_in * lax.rsqrt(mean_sq + 1e-06) * gain_vector
 
 
+QUERY_BLOCK = 128
+KEY_BLOCK = 512
+
+
+def attend_kernel(len_ref, q_ref, pre_ref, cache_ref, nk_ref, nv_ref, out_ref, score_ref):
+    block = pl.program_id(0)
+    length = len_ref[0]
+    queries = q_ref[...]
+    scale = HD ** (-0.5)
+    prefix_chunks = pre_ref.shape[0] // KEY_BLOCK
+    cache_chunks = cache_ref.shape[0] // KEY_BLOCK
+    row_ids = block * QUERY_BLOCK + lax.broadcasted_iota(jnp.int32, (QUERY_BLOCK, KEY_BLOCK), 0)
+    col_ids = lax.broadcasted_iota(jnp.int32, (QUERY_BLOCK, KEY_BLOCK), 1)
+
+    def keys_of(chunk):
+        if chunk < prefix_chunks:
+            return pre_ref[pl.ds(chunk * KEY_BLOCK, KEY_BLOCK), pl.ds(0, HD)]
+        if chunk < prefix_chunks + cache_chunks:
+            start = (chunk - prefix_chunks) * KEY_BLOCK
+            return cache_ref[pl.ds(start, KEY_BLOCK), pl.ds(0, HD)]
+        return nk_ref[...]
+
+    def values_of(chunk):
+        if chunk < prefix_chunks:
+            return pre_ref[pl.ds(chunk * KEY_BLOCK, KEY_BLOCK), pl.ds(HD, HD)]
+        if chunk < prefix_chunks + cache_chunks:
+            start = (chunk - prefix_chunks) * KEY_BLOCK
+            return cache_ref[pl.ds(start, KEY_BLOCK), pl.ds(HD, HD)]
+        return nv_ref[...]
+
+    def visible_of(chunk):
+        if chunk < prefix_chunks:
+            return None
+        if chunk < prefix_chunks + cache_chunks:
+            return col_ids + (chunk - prefix_chunks) * KEY_BLOCK < length
+        return col_ids <= row_ids
+
+    chunks = prefix_chunks + cache_chunks + 1
+    row_peak = None
+    for chunk in range(chunks):
+        part = lax.dot_general(
+            queries, keys_of(chunk), (((1,), (1,)), ((), ())),
+            preferred_element_type=jnp.float32,
+        ) * scale
+        visible = visible_of(chunk)
+        if visible is not None:
+            part = jnp.where(visible, part, -1e30)
+        score_ref[:, pl.ds(chunk * KEY_BLOCK, KEY_BLOCK)] = part
+        peak = jnp.max(part, -1, keepdims=True)
+        row_peak = peak if row_peak is None else jnp.maximum(row_peak, peak)
+    denominator = jnp.zeros((QUERY_BLOCK, 1), jnp.float32)
+    weighted = jnp.zeros((QUERY_BLOCK, HD), jnp.float32)
+    for chunk in range(chunks):
+        weights = jnp.exp(score_ref[:, pl.ds(chunk * KEY_BLOCK, KEY_BLOCK)] - row_peak)
+        visible = visible_of(chunk)
+        if visible is not None:
+            weights = jnp.where(visible, weights, 0.0)
+        denominator = denominator + jnp.sum(weights, -1, keepdims=True)
+        weighted = weighted + jnp.dot(
+            weights.astype(jnp.bfloat16), values_of(chunk), preferred_element_type=jnp.float32
+        )
+    out_ref[...] = (weighted / denominator).astype(out_ref.dtype)
+
+
+def attend(cache_lens, queries, prefix_pairs, cache_pairs, keys_new, values_new):
+    new_rows = queries.shape[0]
+    whole = lambda block, lens: (0, 0)
+    rows = lambda block, lens: (block, 0)
+    chunks = (prefix_pairs.shape[0] + cache_pairs.shape[0]) // KEY_BLOCK + 1
+    return pl.pallas_call(
+        attend_kernel,
+        grid_spec=pltpu.PrefetchScalarGridSpec(
+            num_scalar_prefetch=1,
+            grid=(new_rows // QUERY_BLOCK,),
+            in_specs=[
+                pl.BlockSpec((QUERY_BLOCK, HD), rows),
+                pl.BlockSpec(prefix_pairs.shape, whole),
+                pl.BlockSpec(cache_pairs.shape, whole),
+                pl.BlockSpec(keys_new.shape, whole),
+                pl.BlockSpec(values_new.shape, whole),
+            ],
+            out_specs=pl.BlockSpec((QUERY_BLOCK, HD), rows),
+            scratch_shapes=[pltpu.VMEM((QUERY_BLOCK, chunks * KEY_BLOCK), jnp.float32)],
+        ),
+        out_shape=jax.ShapeDtypeStruct((new_rows, HD), jnp.bfloat16),
+        compiler_params=pltpu.CompilerParams(dimension_semantics=("arbitrary",)),
+    )(cache_lens, queries, prefix_pairs, cache_pairs, keys_new, values_new)
+
+
 def layer(
     tokens,
     w_q,
@@ -48,7 +137,6 @@
     cache_rows,
 ):
     heads_local = w_q.shape[1] // HD
-    width_local = heads_local * HD
     tp_size = lax.axis_size("tp")
     flat_rows = lax.all_to_all(
         jnp.broadcast_to(tokens, (tp_size,) + tokens.shape[1:]), "tp", 0, 0, tiled=True
@@ -70,42 +158,22 @@
     v_new = values_new.reshape(NEW, heads_local, HD).astype(jnp.bfloat16)
     appended = jnp.stack([k_rot, v_new], axis=2).reshape(1, NEW, heads_local * 2 * HD)
 
-    shared = chosen.reshape(-1, heads_local, 2, HD)
-    cached = cache_rows[0].reshape(-1, heads_local, 2, HD)
-    row_ids = jnp.arange(NEW, dtype=jnp.int32)
-    columns = jnp.arange(cached.shape[0], dtype=jnp.int32)
-    blocks = (
-        (shared[:, :, 0], shared[:, :, 1], None),
-        (cached[:, :, 0], cached[:, :, 1], (columns < length)[None, :]),
-        (k_rot, v_new, row_ids[None, :] <= row_ids[:, None]),
-    )
-    scores = []
-    for keys_block, _, visible in blocks:
-        part = jnp.einsum(
-            "qhd,khd->hqk", q_rot, keys_block, preferred_element_type=jnp.float32
-        ) * HD ** (-0.5)
-        if visible is not None:
-            part = jnp.where(visible[None], part, -1e30)
-        scores.append(part)
-    row_peak = functools.reduce(jnp.maximum, [jnp.max(part, -1) for part in scores])
-    denominator = 0.0
-    weighted = 0.0
-    for (_, values_block, visible), part in zip(blocks, scores):
-        weights = jnp.exp(part - row_peak[..., None])
-        if visible is not None:
-            weights = jnp.where(visible[None], weights, 0.0)
-        denominator = denominator + jnp.sum(weights, -1)
-        weighted = weighted + jnp.einsum(
-            "hqk,khd->hqd",
-            weights.astype(jnp.bfloat16),
-            values_block,
-            preferred_element_type=jnp.float32,
+    shared = chosen.reshape(-1, heads_local * 2 * HD)
+    cached = cache_rows[0]
+    heads_out = []
+    for head in range(heads_local):
+        pair = slice(head * 2 * HD, (head + 1) * 2 * HD)
+        heads_out.append(
+            attend(
+                cache_lens,
+                q_rot[:, head],
+                shared[:, pair],
+                cached[:, pair],
+                k_rot[:, head],
+                v_new[:, head],
+            )
         )
-    attended = (
-        jnp.transpose(weighted / denominator[..., None], (1, 0, 2))
-        .reshape(NEW, width_local)
-        .astype(jnp.bfloat16)
-    )
+    attended = jnp.concatenate(heads_out, -1)
     partial_out = jnp.dot(attended, w_o, preferred_element_type=jnp.float32)
     blocks_out = partial_out.astype(jnp.bfloat16).reshape(tp_size, -1, partial_out.shape[1])
     mine = jnp.sum(lax.all_to_all(blocks_out, "tp", 0, 0, tiled=True).astype(jnp.float32), 0)

time: 140 us -> 139 us (level)
  matrix products: 19.3 us -> 8.09 us
  Pallas kernels: 0 us -> 9.1 us
  waiting for transfers between devices: 59 us -> 63.5 us
  local copies, waits for them, and re-layouts: 10.1 us -> 6.71 us
    dot_general x5 -> x0, matrix products: 12.7 us -> none  [the longest x3 6.61 us: layer(): jnp.einsum('qhd,khd->hqk', q_rot, keys_block, preferred_element_type=jnp....]
    pallas_call x0 -> x1, Pallas kernels: none -> 9.1 us  [attend(): pl.pallas_call(attend_kernel, grid_spec=pltpu.PrefetchScalarGridSpec(num_...]
    unnamed x30 -> x21, local copies, waits for them, and re-layouts: 6.04 us -> 1.68 us
    all_to_all x1, waiting for transfers between devices: 20.5 us -> 24.7 us  [layer(): lax.all_to_all(jnp.broadcast_to(tokens, (tp_size,) + tokens.shape[1:]), '...]
    reduce_sum x3 -> x0, other arithmetic: 3.23 us -> none  [layer(): denominator = denominator + jnp.sum(weights, -1)]
    dot_general x0 -> x2, local copies, waits for them, and re-layouts: none -> 1.67 us  [the longest x1 0.84 us: layer(): queries = jnp.dot(flat_rows, w_q, preferred_element_type=jnp.float32)]
    concatenate x0 -> x2, other arithmetic: none -> 1.53 us  [rotate(): jnp.concatenate([first_half * cosine - second_half * sine_part, second_ha...]
  transfers between devices with their start and end apart: 3 -> 3, of which waited for: 3 -> 3; matrix products, arithmetic and copies ran while one was open for 13% -> 10% of each run, Pallas kernels for 0% -> 0%
where the time goes in v5:
time: 139 us
  waiting for transfers between devices  63.5 us (46%)
  starting transfers between devices  29.3 us (21%)
  blocking collectives  13.1 us (9%)
  Pallas kernels  9.1 us (7%)
  matrix products  8.09 us (6%)
  other arithmetic  7.49 us (5%)
  local copies, waits for them, and re-layouts  6.71 us (5%)
  between operations  1.47 us (1%)
    all_to_all x1, waiting for transfers between devices, layer(): lax.all_to_all(blocks_out, 'tp', 0, 0, tiled=True).astype(jnp.float32)  30 us
    all_to_all x1, waiting for transfers between devices, layer(): lax.all_to_all(jnp.broadcast_to(tokens, (tp_size,) + tokens.shape[1:]), '...  24.7 us
    all_to_all x1, starting transfers between devices, layer(): chosen = lax.all_to_all(outgoing, 'req', 0, 0, tiled=True)  19.6 us
    psum x1, blocking collectives, layer(): lax.psum((jnp.sum(queries * queries, -1), jnp.sum(keys_new * keys_new, -1...  13.1 us
    pallas_call x1, Pallas kernels, attend(): pl.pallas_call(attend_kernel, grid_spec=pltpu.PrefetchScalarGridSpec(num_...  9.1 us
    all_to_all x1, waiting for transfers between devices, layer(): chosen = lax.all_to_all(outgoing, 'req', 0, 0, tiled=True)  8.84 us
    all_to_all x1, starting transfers between devices, layer(): lax.all_to_all(jnp.broadcast_to(tokens, (tp_size,) + tokens.shape[1:]), '...  5.36 us
    all_to_all x1, starting transfers between devices, layer(): lax.all_to_all(blocks_out, 'tp', 0, 0, tiled=True).astype(jnp.float32)  4.38 us
  transfers between devices with their start and end apart: 3, of which 3 were waited for; matrix products, arithmetic and copies ran while one was open for 10% of the time, Pallas kernels for 0%

profile of v5, /device:TPU:39, one launch (start us, length us, event | category | flops | bytes accessed | tf_op | source)
XLA Modules:
  0.0 138.7 jit_solution(2942392632967709781)
XLA Ops:
  0.6 2.6 %broadcast_in_dim.17 = bf16[8,64,2048]{2,1,0:T(8,128)(2,1)} broadcast(bf16[64,2048]{1,0:T(8,128)(2,1)} %bitcast.47), dimensions={1,2} | broadcast | bytes 2359296 | tf_op jit(solution)/shard_map/broadcast_in_dim | solution.py:142
  3.3 5.4 %all-to-all-start = ((bf16[8,64,2048]{2,1,0:T(8,128)(2,1)}), bf16[8,64,2048]{2,1,0:T(8,128)(2,1)S(1)}, u32[]{:S(2)}, u32[]{:S(2)}) async-start(bf16[8,64,2048]{2,1,0:T(8,128)(2,1)} %broadcast_in_dim.17), calls=%async_computation | async-start | bytes 4194304 | tf_op jit(solution)/shard_map/all_to_all | solution.py:141
  10.0 0.9 broadcast_select_fusion
  10.9 24.7 %all-to-all-done = bf16[8,64,2048]{2,1,0:T(8,128)(2,1)S(1)} async-done(((bf16[8,64,2048]{2,1,0:T(8,128)(2,1)}), bf16[8,64,2048]{2,1,0:T(8,128)(2,1)S(1)}, u32[]{:S(2)}, u32[]{:S(2)}) %all-to-all-start) | async-done | bytes 2097184 | tf_op jit(solution)/shard_map/all_to_all | solution.py:141
  35.6 19.6 %all-to-all-start.1 = ((bf16[64,16,256]{2,1,0:T(8,128)(2,1)}), bf16[64,16,256]{2,1,0:T(8,128)(2,1)S(1)}, u32[]{:S(2)}, u32[]{:S(2)}) async-start(bf16[64,16,256]{2,1,0:T(8,128)(2,1)} %broadcast_select_fusion), calls=%async_computation.1 | async-start | bytes 1048576 | tf_op jit(solution)/shard_map/all_to_all | solution.py:145
  55.2 1.9 %multiply_reduce_fusion.2 = (f32[512]{0:T(512)S(1)}, f32[512,128]{0,1:T(8,128)S(1)}) fusion(bf16[512,2048]{1,0:T(8,128)(2,1)S(1)} %bitcast.36, bf16[2048,128]{1,0:T(8,128)(2,1)} %param.13), kind=kOutput, calls=%fused_computation.32 | convolution fusion | flops 268566016 | bytes 2885632 | tf_op jit(solution)/shard_map/dot_general | solution.py:146
  57.0 0.8 copy.17
  57.9 1.9 %multiply_reduce_fusion.1 = (f32[512]{0:T(512)S(1)}, f32[512,128]{0,1:T(8,128)S(1)}) fusion(bf16[512,2048]{1,0:T(8,128)(2,1)S(1)} %bitcast.37, bf16[2048,128]{1,0:T(8,128)(2,1)} %param.14), kind=kOutput, calls=%fused_computation.30 | convolution fusion | flops 268566016 | bytes 2885632 | tf_op jit(solution)/shard_map/dot_general | solution.py:147
  59.8 0.8 copy.18
  60.6 13.1 %all-reduce = (f32[512]{0:T(512)S(1)}, f32[512]{0:T(512)S(1)}) all-reduce(f32[512]{0:T(512)S(1)} %get-tuple-element.12, f32[512]{0:T(512)S(1)} %get-tuple-element.14), channel_id=1, replica_groups=mesh['req'=64,'tp'=8] {'tp'}, use_global_device_ids=true, to_apply=%region_1.2 | all-reduce | flops 1024 | bytes 8192 | tf_op jit(solution)/shard_map/psum | solution.py:149
  73.7 1.1 multiply_bitcast_fusion.1
  74.9 1.1 multiply_bitcast_fusion
  76.0 1.3 fusion.16
  77.3 0.8 pad_maximum_fusion.2.nk_ref
  78.0 0.8 pad_maximum_fusion.1.q_ref
  78.8 1.4 convolution_convert_fusion.1.nv_ref
  80.2 8.8 %all-to-all-done.1 = bf16[64,16,256]{2,1,0:T(8,128)(2,1)S(1)} async-done(((bf16[64,16,256]{2,1,0:T(8,128)(2,1)}), bf16[64,16,256]{2,1,0:T(8,128)(2,1)S(1)}, u32[]{:S(2)}, u32[]{:S(2)}) %all-to-all-start.1) | async-done | bytes 524320 | tf_op jit(solution)/shard_map/all_to_all | solution.py:145
  89.0 0.8 copy-done.2
  89.8 9.1 %shard_map.131 = bf16[512,128]{1,0:T(8,128)(2,1)} custom-call(s32[1]{0:T(128)S(6)} %copy.23.len_ref, bf16[512,128]{1,0:T(8,128)(2,1)} %pad_maximum_fusion.1.q_ref, bf16[1024,256]{1,0:T(8,128)(2,1)} %bitcast.41, bf16[4096,256]{1,0:T(8,128)(2,1)} %bitcast.40, bf16[512,128]{1,0:T(8,128)(2,1)} %pad_maximum_fusion.2.nk_ref, ...), custom_call_target="tpu_custom_call" | custom-call | tf_op jit(solution)/shard_map/pallas_call | solution.py:105
  98.9 3.0 %convolution_convert_fusion = bf16[512,2048]{1,0:T(8,128)(2,1)} fusion(bf16[512,128]{1,0:T(8,128)(2,1)} %shard_map.131, bf16[128,2048]{1,0:T(8,128)(2,1)S(1)} %copy-done), kind=kOutput, calls=%fused_computation.2 | convolution fusion | flops 269484032 | bytes 2752512 | tf_op jit(solution)/shard_map/dot_general | solution.py:177
  101.9 4.4 %all-to-all-start.2 = ((bf16[8,64,2048]{2,1,0:T(8,128)(2,1)}), bf16[8,64,2048]{2,1,0:T(8,128)(2,1)S(1)}, u32[]{:S(2)}, u32[]{:S(2)}) async-start(bf16[8,64,2048]{2,1,0:T(8,128)(2,1)} %bitcast.39), calls=%async_computation.2 | async-start | bytes 4194304 | tf_op jit(solution)/shard_map/all_to_all | solution.py:179
  106.5 0.8 copy.21
  107.4 30.0 %all-to-all-done.2 = bf16[8,64,2048]{2,1,0:T(8,128)(2,1)S(1)} async-done(((bf16[8,64,2048]{2,1,0:T(8,128)(2,1)}), bf16[8,64,2048]{2,1,0:T(8,128)(2,1)S(1)}, u32[]{:S(2)}, u32[]{:S(2)}) %all-to-all-start.2) | async-done | bytes 2097184 | tf_op jit(solution)/shard_map/all_to_all | solution.py:179
  137.9 0.9 fusion.2
  (31 shorter events, 1.4 us)
Async XLA Ops:
  0.6 98.3 %copy-start = (bf16[128,2048]{1,0:T(8,128)(2,1)S(1)}, bf16[128,2048]{1,0:T(8,128)(2,1)}, u32[]{:S(2)}) copy-start(bf16[128,2048]{1,0:T(8,128)(2,1)} %param.16) | copy-start | bytes 1572868
  3.3 6.0 %copy-start.9 = (s32[64]{0:T(128)S(1)}, s32[64]{0:T(128)}, u32[]{:S(2)}) copy-start(s32[64]{0:T(128)} %param.21) | copy-start | bytes 772
  3.3 6.0 %copy-start.1 = (bf16[8,16,256]{2,1,0:T(8,128)(2,1)S(1)}, bf16[8,16,256]{2,1,0:T(8,128)(2,1)}, u32[]{:S(2)}) copy-start(bf16[8,16,256]{2,1,0:T(8,128)(2,1)} %param.22) | copy-start | bytes 196612
  3.3 32.3 %all-to-all-start = ((bf16[8,64,2048]{2,1,0:T(8,128)(2,1)}), bf16[8,64,2048]{2,1,0:T(8,128)(2,1)S(1)}, u32[]{:S(2)}, u32[]{:S(2)}) async-start(bf16[8,64,2048]{2,1,0:T(8,128)(2,1)} %broadcast_in_dim.17), calls=%async_computation | async-start | bytes 4194304 | tf_op jit(solution)/shard_map/all_to_all | solution.py:141
  35.6 53.4 %all-to-all-start.1 = ((bf16[64,16,256]{2,1,0:T(8,128)(2,1)}), bf16[64,16,256]{2,1,0:T(8,128)(2,1)S(1)}, u32[]{:S(2)}, u32[]{:S(2)}) async-start(bf16[64,16,256]{2,1,0:T(8,128)(2,1)} %broadcast_select_fusion), calls=%async_computation.1 | async-start | bytes 1048576 | tf_op jit(solution)/shard_map/all_to_all | solution.py:145
  57.0 16.7 %copy-start.7 = (f32[128]{0:T(128)S(1)}, f32[128]{0:T(128)}, u32[]{:S(2)}) copy-start(f32[128]{0:T(128)} %param.17) | copy-start | bytes 1540
  57.9 17.0 %copy-start.8 = (f32[128]{0:T(128)S(1)}, f32[128]{0:T(128)}, u32[]{:S(2)}) copy-start(f32[128]{0:T(128)} %param.18) | copy-start | bytes 1540
  73.7 5.1 %copy-start.5 = (bf16[2048,128]{1,0:T(8,128)(2,1)S(1)}, bf16[2048,128]{1,0:T(8,128)(2,1)}, u32[]{:S(2)}) copy-start(bf16[2048,128]{1,0:T(8,128)(2,1)} %param.15) | copy-start | bytes 1572868
  89.0 0.8 copy-start.2
  101.9 4.4 %copy-start.3 = (bf16[512,128]{1,0:T(8,128)(2,1)S(1)}, bf16[512,128]{1,0:T(8,128)(2,1)}, u32[]{:S(2)}) copy-start(bf16[512,128]{1,0:T(8,128)(2,1)} %convolution_convert_fusion.1.nv_ref) | copy-start | bytes 393220
  101.9 35.5 %all-to-all-start.2 = ((bf16[8,64,2048]{2,1,0:T(8,128)(2,1)}), bf16[8,64,2048]{2,1,0:T(8,128)(2,1)S(1)}, u32[]{:S(2)}, u32[]{:S(2)}) async-start(bf16[8,64,2048]{2,1,0:T(8,128)(2,1)} %bitcast.39), calls=%async_computation.2 | async-start | bytes 4194304 | tf_op jit(solution)/shard_map/all_to_all | solution.py:179
  106.4 31.5 %copy-start.4 = (bf16[1,64,2048]{2,1,0:T(8,128)(2,1)S(1)}, bf16[1,64,2048]{2,1,0:T(8,128)(2,1)}, u32[]{:S(2)}) copy-start(bf16[1,64,2048]{2,1,0:T(8,128)(2,1)} %param.12) | copy-start | bytes 786436
  106.4 31.5 %copy-start.6 = (f32[2048]{0:T(1024)S(1)}, f32[2048]{0:T(1024)}, u32[]{:S(2)}) copy-start(f32[2048]{0:T(1024)} %param.19) | copy-start | bytes 24580

commit v6 on v5

--- a/solution.py
+++ b/solution.py
@@ -3,7 +3,7 @@
 from jax import lax
 from jax.experimental import pallas as pl
 from jax.experimental.pallas import tpu as pltpu
-from jax.sharding import PartitionSpec as P
+from jax.sharding import Mesh, PartitionSpec as P
 
 HEADS = 8
 HD = 128
@@ -122,6 +122,25 @@
     )(cache_lens, queries, prefix_pairs, cache_pairs, keys_new, values_new)
 
 
+REQ_AXES = ("req_hi", "req_mid", "req_lo")
+
+
+def exchange_prefix(prefix_cache, group_ids):
+    hi, mid, lo = (lax.axis_size(name) for name in REQ_AXES)
+    rows, width = prefix_cache.shape[1:]
+    dest = (
+        jnp.arange(hi)[:, None, None] * (mid * lo)
+        + jnp.arange(lo)[None, :, None]
+        + jnp.arange(mid)[None, None, :] * lo
+    ).reshape(-1)
+    outgoing = jnp.take(prefix_cache, jnp.take(group_ids, dest), axis=0)
+    first = lax.all_to_all(outgoing, ("req_hi", "req_lo"), 0, 0, tiled=True)
+    first = first.reshape(hi * lo, mid, rows, width).transpose(1, 0, 2, 3)
+    second = lax.all_to_all(first.reshape(-1, rows, width), "req_mid", 0, 0, tiled=True)
+    second = second.reshape(mid, hi, lo, rows, width).transpose(1, 0, 2, 3, 4)
+    return second.reshape(-1, width)
+
+
 def layer(
     tokens,
     w_q,
@@ -141,8 +160,7 @@
     flat_rows = lax.all_to_all(
         jnp.broadcast_to(tokens, (tp_size,) + tokens.shape[1:]), "tp", 0, 0, tiled=True
     ).reshape(-1, tokens.shape[2])
-    outgoing = jnp.take(prefix_cache, group_ids, axis=0)
-    chosen = lax.all_to_all(outgoing, "req", 0, 0, tiled=True)
+    chosen = exchange_prefix(prefix_cache, group_ids)
     queries = jnp.dot(flat_rows, w_q, preferred_element_type=jnp.float32)
     keys_new = jnp.dot(flat_rows, w_k, preferred_element_type=jnp.float32)
     values_new = jnp.dot(flat_rows, w_v, preferred_element_type=jnp.float32)
@@ -150,7 +168,7 @@
     full_width = HEADS * HD
     queries = queries * lax.rsqrt(square_sums[0] / full_width + 1e-06)[:, None] * q_gain
     keys_new = keys_new * lax.rsqrt(square_sums[1] / full_width + 1e-06)[:, None] * k_gain
-    prefix_len = prefix_cache.shape[1] * lax.axis_size("req")
+    prefix_len = prefix_cache.shape[1] * lax.axis_size(REQ_AXES)
     length = cache_lens[0]
     positions = (prefix_len + length + jnp.arange(NEW, dtype=jnp.int32)).astype(jnp.float32)
     q_rot = rotate(queries.reshape(NEW, heads_local, HD), positions).astype(jnp.bfloat16)
@@ -182,11 +200,19 @@
 
 
 def solution(mesh):
+    req_size = mesh.shape["req"]
+    lo = 2 if req_size % 2 == 0 else 1
+    mid = 16 if (req_size // lo) % 16 == 0 else req_size // lo
+    hi = req_size // (lo * mid)
+    split_mesh = Mesh(
+        mesh.devices.reshape(hi, mid, lo, mesh.shape["tp"]), REQ_AXES + ("tp",)
+    )
+    req = REQ_AXES
     return jax.shard_map(
         layer,
-        mesh=mesh,
+        mesh=split_mesh,
         in_specs=(
-            P("req", "tp", None),
+            P(req, "tp", None),
             P(None, "tp"),
             P(None, "tp"),
             P(None, "tp"),
@@ -194,11 +220,11 @@
             P("tp"),
             P("tp"),
             P(),
-            P("req"),
+            P(req),
             P(),
-            P(None, "req", "tp"),
-            P("req", None, "tp"),
+            P(None, req, "tp"),
+            P(req, None, "tp"),
         ),
-        out_specs=(P("req", "tp", None), P("req", None, "tp")),
+        out_specs=(P(req, "tp", None), P(req, None, "tp")),
         check_vma=False,
     )

time: 139 us -> 140 us (level)
  the two profiles are of different devices: /device:TPU:39 before, /device:TPU:1 now
where the time goes in v6:
time: 140 us; the launch traced here: 139 us
  waiting for transfers between devices  51.4 us (37%)
  blocking collectives  33.7 us (24%)
  starting transfers between devices  19.4 us (14%)
  Pallas kernels  9.11 us (7%)
  local copies, waits for them, and re-layouts  9.01 us (6%)
  matrix products  8.07 us (6%)
  other arithmetic  6.86 us (5%)
  between operations  1.5 us (1%)
    all_to_all x1, waiting for transfers between devices, layer(): lax.all_to_all(blocks_out, 'tp', 0, 0, tiled=True).astype(jnp.float32)  25.8 us
    all_to_all x1, waiting for transfers between devices, layer(): lax.all_to_all(jnp.broadcast_to(tokens, (tp_size,) + tokens.shape[1:]), '...  25.5 us
    all_to_all x1, blocking collectives, exchange_prefix(): first = lax.all_to_all(outgoing, ('req_hi', 'req_lo'), 0, 0, tiled=True)  18.5 us
    psum x1, blocking collectives, layer(): lax.psum((jnp.sum(queries * queries, -1), jnp.sum(keys_new * keys_new, -1...  15.2 us
    all_to_all x1, starting transfers between devices, exchange_prefix(): lax.all_to_all(first.reshape(-1, rows, width), 'req_mid', 0, 0, tiled=True)  12 us
    pallas_call x1, Pallas kernels, attend(): pl.pallas_call(attend_kernel, grid_spec=pltpu.PrefetchScalarGridSpec(num_...  9.11 us
    all_to_all x1, starting transfers between devices, layer(): lax.all_to_all(blocks_out, 'tp', 0, 0, tiled=True).astype(jnp.float32)  3.73 us
    all_to_all x1, starting transfers between devices, layer(): lax.all_to_all(jnp.broadcast_to(tokens, (tp_size,) + tokens.shape[1:]), '...  3.6 us
  transfers between devices with their start and end apart: 3, of which 2 were waited for; matrix products, arithmetic and copies ran while one was open for 10% of the time, Pallas kernels for 0%

profile of v6, /device:TPU:1, one launch (start us, length us, event | category | flops | bytes accessed | tf_op | source)
XLA Modules:
  0.0 139.0 jit_solution(3569644986500833340)
XLA Ops:
  1.0 1.4 %gather_fusion = s32[64]{0:T(128)S(1)} fusion(s32[64]{0:T(128)} %param.21, s32[1024]{0:T(1024)S(1)} %pad_clamp_fusion.1), kind=kCustom, calls=%fused_computation | custom fusion | bytes 768 | tf_op jit(solution)/shard_map/jit(_take)/gather | solution.py:136
  2.5 1.4 %gather_fusion.1 = bf16[64,16,256]{2,1,0:T(8,128)(2,1)S(1)} fusion(bf16[8,16,256]{2,1,0:T(8,128)(2,1)} %param.22, s32[1024]{0:T(1024)S(1)} %pad_clamp_fusion), kind=kCustom, calls=%fused_computation.1 | custom fusion | bytes 1048832 | tf_op jit(solution)/shard_map/jit(_take)/gather | solution.py:136
  4.1 18.5 %all_to_all.20 = bf16[64,16,256]{2,1,0:T(8,128)(2,1)S(1)} all-to-all(bf16[64,16,256]{2,1,0:T(8,128)(2,1)S(1)} %broadcast_select_fusion), channel_id=1, replica_groups=mesh['req_hi'=2,'req_mid'=16,'req_lo'=2,'tp'=8] {'req_hi','req_lo'}, dimensions={0} | all-to-all | bytes 1048576 | tf_op jit(solution)/shard_map/all_to_all | solution.py:137
  22.6 1.6 %broadcast_in_dim.23 = bf16[8,64,2048]{2,1,0:T(8,128)(2,1)} broadcast(bf16[64,2048]{1,0:T(8,128)(2,1)S(1)} %bitcast.64), dimensions={1,2} | broadcast | bytes 2359296 | tf_op jit(solution)/shard_map/broadcast_in_dim | solution.py:161
  24.2 3.6 %all-to-all-start = ((bf16[8,64,2048]{2,1,0:T(8,128)(2,1)}), bf16[8,64,2048]{2,1,0:T(8,128)(2,1)S(1)}, u32[]{:S(2)}, u32[]{:S(2)}) async-start(bf16[8,64,2048]{2,1,0:T(8,128)(2,1)} %broadcast_in_dim.23), calls=%async_computation | async-start | bytes 4194304 | tf_op jit(solution)/shard_map/all_to_all | solution.py:160
  28.5 0.8 copy.24
  29.3 25.5 %all-to-all-done = bf16[8,64,2048]{2,1,0:T(8,128)(2,1)S(1)} async-done(((bf16[8,64,2048]{2,1,0:T(8,128)(2,1)}), bf16[8,64,2048]{2,1,0:T(8,128)(2,1)S(1)}, u32[]{:S(2)}, u32[]{:S(2)}) %all-to-all-start) | async-done | bytes 2097184 | tf_op jit(solution)/shard_map/all_to_all | solution.py:160
  54.8 12.0 %all-to-all-start.2 = ((bf16[64,16,256]{2,1,0:T(8,128)(2,1)}), bf16[64,16,256]{2,1,0:T(8,128)(2,1)S(1)}, u32[]{:S(2)}, u32[]{:S(2)}) async-start(bf16[64,16,256]{2,1,0:T(8,128)(2,1)} %bitcast.11), calls=%async_computation.2 | async-start | bytes 1048576 | tf_op jit(solution)/shard_map/all_to_all | solution.py:139
  66.9 1.9 %multiply_reduce_fusion.2 = (f32[512]{0:T(512)S(1)}, f32[512,128]{0,1:T(8,128)S(1)}) fusion(bf16[512,2048]{1,0:T(8,128)(2,1)S(1)} %bitcast.51, bf16[2048,128]{1,0:T(8,128)(2,1)} %param.13), kind=kOutput, calls=%fused_computation.33 | convolution fusion | flops 268566016 | bytes 2885632 | tf_op jit(solution)/shard_map/dot_general | solution.py:164
  68.7 0.8 copy.23
  69.6 1.9 %multiply_reduce_fusion.1 = (f32[512]{0:T(512)S(1)}, f32[512,128]{0,1:T(8,128)S(1)}) fusion(bf16[512,2048]{1,0:T(8,128)(2,1)S(1)} %bitcast.52, bf16[2048,128]{1,0:T(8,128)(2,1)} %param.14), kind=kOutput, calls=%fused_computation.31 | convolution fusion | flops 268566016 | bytes 2885632 | tf_op jit(solution)/shard_map/dot_general | solution.py:165
  71.5 0.8 copy.26
  72.3 15.2 %all-reduce = (f32[512]{0:T(512)S(1)}, f32[512]{0:T(512)S(1)}) all-reduce(f32[512]{0:T(512)S(1)} %get-tuple-element.14, f32[512]{0:T(512)S(1)} %get-tuple-element.16), channel_id=1, replica_groups=mesh['req_hi'=2,'req_mid'=16,'req_lo'=2,'tp'=8] {'tp'}, use_global_device_ids=true, to_apply=%region_1.2 | all-reduce | flops 1024 | bytes 8192 | tf_op jit(solution)/shard_map/psum | solution.py:167
  87.6 1.1 multiply_bitcast_fusion.1
  88.7 1.1 multiply_bitcast_fusion
  89.8 1.3 fusion.16
  92.6 1.4 convolution_convert_fusion.1.nv_ref
  94.0 0.8 copy.25
  94.9 9.1 %shard_map.131 = bf16[512,128]{1,0:T(8,128)(2,1)} custom-call(s32[1]{0:T(128)S(6)} %copy.31.len_ref, bf16[512,128]{1,0:T(8,128)(2,1)} %pad_maximum_fusion.1.q_ref, bf16[1024,256]{1,0:T(8,128)(2,1)} %bitcast.58, bf16[4096,256]{1,0:T(8,128)(2,1)} %bitcast.55, bf16[512,128]{1,0:T(8,128)(2,1)} %pad_maximum_fusion.2.nk_ref, ...), custom_call_target="tpu_custom_call" | custom-call | tf_op jit(solution)/shard_map/pallas_call | solution.py:105
  104.0 2.9 %convolution_convert_fusion = bf16[512,2048]{1,0:T(8,128)(2,1)} fusion(bf16[512,128]{1,0:T(8,128)(2,1)} %shard_map.131, bf16[128,2048]{1,0:T(8,128)(2,1)S(1)} %copy-done), kind=kOutput, calls=%fused_computation.3 | convolution fusion | flops 269484032 | bytes 2752512 | tf_op jit(solution)/shard_map/dot_general | solution.py:195
  106.9 3.7 %all-to-all-start.3 = ((bf16[8,64,2048]{2,1,0:T(8,128)(2,1)}), bf16[8,64,2048]{2,1,0:T(8,128)(2,1)S(1)}, u32[]{:S(2)}, u32[]{:S(2)}) async-start(bf16[8,64,2048]{2,1,0:T(8,128)(2,1)} %bitcast.54), calls=%async_computation.3 | async-start | bytes 4194304 | tf_op jit(solution)/shard_map/all_to_all | solution.py:197
  110.9 0.8 copy.29
  111.8 25.8 %all-to-all-done.3 = bf16[8,64,2048]{2,1,0:T(8,128)(2,1)S(1)} async-done(((bf16[8,64,2048]{2,1,0:T(8,128)(2,1)}), bf16[8,64,2048]{2,1,0:T(8,128)(2,1)S(1)}, u32[]{:S(2)}, u32[]{:S(2)}) %all-to-all-start.3) | async-done | bytes 2097184 | tf_op jit(solution)/shard_map/all_to_all | solution.py:197
  138.1 0.9 fusion.2
  (39 shorter events, 2.9 us)
Async XLA Ops:
  0.6 103.3 %copy-start = (bf16[128,2048]{1,0:T(8,128)(2,1)S(1)}, bf16[128,2048]{1,0:T(8,128)(2,1)}, u32[]{:S(2)}) copy-start(bf16[128,2048]{1,0:T(8,128)(2,1)} %param.16) | copy-start | bytes 1572868
  0.6 21.9 %copy-start.2 = (bf16[1,64,2048]{2,1,0:T(8,128)(2,1)S(1)}, bf16[1,64,2048]{2,1,0:T(8,128)(2,1)}, u32[]{:S(2)}) copy-start(bf16[1,64,2048]{2,1,0:T(8,128)(2,1)} %param.12) | copy-start | bytes 786436
  24.2 30.7 %all-to-all-start = ((bf16[8,64,2048]{2,1,0:T(8,128)(2,1)}), bf16[8,64,2048]{2,1,0:T(8,128)(2,1)S(1)}, u32[]{:S(2)}, u32[]{:S(2)}) async-start(bf16[8,64,2048]{2,1,0:T(8,128)(2,1)} %broadcast_in_dim.23), calls=%async_computation | async-start | bytes 4194304 | tf_op jit(solution)/shard_map/all_to_all | solution.py:160
  54.8 39.2 %all-to-all-start.2 = ((bf16[64,16,256]{2,1,0:T(8,128)(2,1)}), bf16[64,16,256]{2,1,0:T(8,128)(2,1)S(1)}, u32[]{:S(2)}, u32[]{:S(2)}) async-start(bf16[64,16,256]{2,1,0:T(8,128)(2,1)} %bitcast.11), calls=%async_computation.2 | async-start | bytes 1048576 | tf_op jit(solution)/shard_map/all_to_all | solution.py:139
  68.7 18.8 %copy-start.6 = (f32[128]{0:T(128)S(1)}, f32[128]{0:T(128)}, u32[]{:S(2)}) copy-start(f32[128]{0:T(128)} %param.17) | copy-start | bytes 1540
  69.6 19.1 %copy-start.7 = (f32[128]{0:T(128)S(1)}, f32[128]{0:T(128)}, u32[]{:S(2)}) copy-start(f32[128]{0:T(128)} %param.18) | copy-start | bytes 1540
  87.6 5.1 %copy-start.4 = (bf16[2048,128]{1,0:T(8,128)(2,1)S(1)}, bf16[2048,128]{1,0:T(8,128)(2,1)}, u32[]{:S(2)}) copy-start(bf16[2048,128]{1,0:T(8,128)(2,1)} %param.15) | copy-start | bytes 1572868
  106.9 3.7 %copy-start.1 = (bf16[512,128]{1,0:T(8,128)(2,1)S(1)}, bf16[512,128]{1,0:T(8,128)(2,1)}, u32[]{:S(2)}) copy-start(bf16[512,128]{1,0:T(8,128)(2,1)} %convolution_convert_fusion.1.nv_ref) | copy-start | bytes 393220
  106.9 30.7 %all-to-all-start.3 = ((bf16[8,64,2048]{2,1,0:T(8,128)(2,1)}), bf16[8,64,2048]{2,1,0:T(8,128)(2,1)S(1)}, u32[]{:S(2)}, u32[]{:S(2)}) async-start(bf16[8,64,2048]{2,1,0:T(8,128)(2,1)} %bitcast.54), calls=%async_computation.3 | async-start | bytes 4194304 | tf_op jit(solution)/shard_map/all_to_all | solution.py:197
  110.8 27.4 %copy-start.3 = (bf16[1,64,2048]{2,1,0:T(8,128)(2,1)S(1)}, bf16[1,64,2048]{2,1,0:T(8,128)(2,1)}, u32[]{:S(2)}) copy-start(bf16[1,64,2048]{2,1,0:T(8,128)(2,1)} %param.12) | copy-start | bytes 786436
  110.8 27.4 %copy-start.5 = (f32[2048]{0:T(1024)S(1)}, f32[2048]{0:T(1024)}, u32[]{:S(2)}) copy-start(f32[2048]{0:T(1024)} %param.19) | copy-start | bytes 24580

commit v7 on v5

--- a/solution.py
+++ b/solution.py
@@ -37,7 +37,7 @@
 KEY_BLOCK = 512
 
 
-def attend_kernel(len_ref, q_ref, pre_ref, cache_ref, nk_ref, nv_ref, out_ref, score_ref):
+def attend_kernel(len_ref, q_ref, pre_ref, cache_ref, nk_ref, nv_ref, wo_ref, out_ref, score_ref):
     block = pl.program_id(0)
     length = len_ref[0]
     queries = q_ref[...]
@@ -65,6 +65,8 @@
 
     def visible_of(chunk):
         if chunk < prefix_chunks:
+            return None
+        if chunk == prefix_chunks:
             return None
         if chunk < prefix_chunks + cache_chunks:
             return col_ids + (chunk - prefix_chunks) * KEY_BLOCK < length
@@ -94,10 +96,13 @@
         weighted = weighted + jnp.dot(
             weights.astype(jnp.bfloat16), values_of(chunk), preferred_element_type=jnp.float32
         )
-    out_ref[...] = (weighted / denominator).astype(out_ref.dtype)
-
-
-def attend(cache_lens, queries, prefix_pairs, cache_pairs, keys_new, values_new):
+    attended = (weighted / denominator).astype(jnp.bfloat16)
+    out_ref[...] = jnp.dot(
+        attended, wo_ref[...], preferred_element_type=jnp.float32
+    ).astype(out_ref.dtype)
+
+
+def attend(cache_lens, queries, prefix_pairs, cache_pairs, keys_new, values_new, w_out):
     new_rows = queries.shape[0]
     whole = lambda block, lens: (0, 0)
     rows = lambda block, lens: (block, 0)
@@ -113,13 +118,14 @@
                 pl.BlockSpec(cache_pairs.shape, whole),
                 pl.BlockSpec(keys_new.shape, whole),
                 pl.BlockSpec(values_new.shape, whole),
+                pl.BlockSpec(w_out.shape, whole),
             ],
-            out_specs=pl.BlockSpec((QUERY_BLOCK, HD), rows),
+            out_specs=pl.BlockSpec((QUERY_BLOCK, w_out.shape[1]), rows),
             scratch_shapes=[pltpu.VMEM((QUERY_BLOCK, chunks * KEY_BLOCK), jnp.float32)],
         ),
-        out_shape=jax.ShapeDtypeStruct((new_rows, HD), jnp.bfloat16),
+        out_shape=jax.ShapeDtypeStruct((new_rows, w_out.shape[1]), jnp.bfloat16),
         compiler_params=pltpu.CompilerParams(dimension_semantics=("arbitrary",)),
-    )(cache_lens, queries, prefix_pairs, cache_pairs, keys_new, values_new)
+    )(cache_lens, queries, prefix_pairs, cache_pairs, keys_new, values_new, w_out)
 
 
 def layer(
@@ -160,21 +166,21 @@
 
     shared = chosen.reshape(-1, heads_local * 2 * HD)
     cached = cache_rows[0]
-    heads_out = []
+    partial_sum = None
     for head in range(heads_local):
         pair = slice(head * 2 * HD, (head + 1) * 2 * HD)
-        heads_out.append(
-            attend(
-                cache_lens,
-                q_rot[:, head],
-                shared[:, pair],
-                cached[:, pair],
-                k_rot[:, head],
-                v_new[:, head],
-            )
+        partial = attend(
+            cache_lens,
+            q_rot[:, head],
+            shared[:, pair],
+            cached[:, pair],
+            k_rot[:, head],
+            v_new[:, head],
+            w_o[head * HD : (head + 1) * HD],
         )
-    attended = jnp.concatenate(heads_out, -1)
-    partial_out = jnp.dot(attended, w_o, preferred_element_type=jnp.float32)
+        partial = partial if heads_local == 1 else partial.astype(jnp.float32)
+        partial_sum = partial if partial_sum is None else partial_sum + partial
+    partial_out = partial_sum.astype(jnp.bfloat16)
     blocks_out = partial_out.astype(jnp.bfloat16).reshape(tp_size, -1, partial_out.shape[1])
     mine = jnp.sum(lax.all_to_all(blocks_out, "tp", 0, 0, tiled=True).astype(jnp.float32), 0)
     hidden = (tokens[0].astype(jnp.float32) + rms_scale(mine, out_gain)).astype(jnp.bfloat16)[None]

time: 139 us -> 138 us (level)
  matrix products: 8.09 us -> 4.1 us
    dot_general x1 -> x0, matrix products: 2.95 us -> none  [layer(): partial_out = jnp.dot(attended, w_o, preferred_element_type=jnp.float32)]
where the time goes in v7:
time: 138 us; the launch traced here: 137 us
  waiting for transfers between devices  64.5 us (47%)
  starting transfers between devices  29.3 us (21%)
  blocking collectives  13.1 us (9%)
  Pallas kernels  10.3 us (7%)
  other arithmetic  7.49 us (5%)
  local copies, waits for them, and re-layouts  6.72 us (5%)
  matrix products  4.1 us (3%)
  between operations  1.47 us (1%)
    all_to_all x1, waiting for transfers between devices, layer(): lax.all_to_all(blocks_out, 'tp', 0, 0, tiled=True).astype(jnp.float32)  30 us
    all_to_all x1, waiting for transfers between devices, layer(): lax.all_to_all(jnp.broadcast_to(tokens, (tp_size,) + tokens.shape[1:]), '...  24.7 us
    all_to_all x1, starting transfers between devices, layer(): chosen = lax.all_to_all(outgoing, 'req', 0, 0, tiled=True)  19.6 us
    psum x1, blocking collectives, layer(): lax.psum((jnp.sum(queries * queries, -1), jnp.sum(keys_new * keys_new, -1...  13.1 us
    pallas_call x1, Pallas kernels, attend(): pl.pallas_call(attend_kernel, grid_spec=pltpu.PrefetchScalarGridSpec(num_...  10.3 us
    all_to_all x1, waiting for transfers between devices, layer(): chosen = lax.all_to_all(outgoing, 'req', 0, 0, tiled=True)  9.87 us
    all_to_all x1, starting transfers between devices, layer(): lax.all_to_all(jnp.broadcast_to(tokens, (tp_size,) + tokens.shape[1:]), '...  5.36 us
    all_to_all x1, starting transfers between devices, layer(): lax.all_to_all(blocks_out, 'tp', 0, 0, tiled=True).astype(jnp.float32)  4.38 us
  transfers between devices with their start and end apart: 3, of which 3 were waited for; matrix products, arithmetic and copies ran while one was open for 10% of the time, Pallas kernels for 0%

profile of v7, /device:TPU:39, one launch (start us, length us, event | category | flops | bytes accessed | tf_op | source)
XLA Modules:
  0.0 137.0 jit_solution(5002780378789400228)
XLA Ops:
  0.6 2.6 %broadcast_in_dim.17 = bf16[8,64,2048]{2,1,0:T(8,128)(2,1)} broadcast(bf16[64,2048]{1,0:T(8,128)(2,1)} %bitcast.45), dimensions={1,2} | broadcast | bytes 2359296 | tf_op jit(solution)/shard_map/broadcast_in_dim | solution.py:148
  3.3 5.4 %all-to-all-start = ((bf16[8,64,2048]{2,1,0:T(8,128)(2,1)}), bf16[8,64,2048]{2,1,0:T(8,128)(2,1)S(1)}, u32[]{:S(2)}, u32[]{:S(2)}) async-start(bf16[8,64,2048]{2,1,0:T(8,128)(2,1)} %broadcast_in_dim.17), calls=%async_computation | async-start | bytes 4194304 | tf_op jit(solution)/shard_map/all_to_all | solution.py:147
  9.3 0.6 gather_fusion
  10.0 0.9 broadcast_select_fusion
  10.9 24.7 %all-to-all-done = bf16[8,64,2048]{2,1,0:T(8,128)(2,1)S(1)} async-done(((bf16[8,64,2048]{2,1,0:T(8,128)(2,1)}), bf16[8,64,2048]{2,1,0:T(8,128)(2,1)S(1)}, u32[]{:S(2)}, u32[]{:S(2)}) %all-to-all-start) | async-done | bytes 2097184 | tf_op jit(solution)/shard_map/all_to_all | solution.py:147
  35.6 19.6 %all-to-all-start.1 = ((bf16[64,16,256]{2,1,0:T(8,128)(2,1)}), bf16[64,16,256]{2,1,0:T(8,128)(2,1)S(1)}, u32[]{:S(2)}, u32[]{:S(2)}) async-start(bf16[64,16,256]{2,1,0:T(8,128)(2,1)} %broadcast_select_fusion), calls=%async_computation.1 | async-start | bytes 1048576 | tf_op jit(solution)/shard_map/all_to_all | solution.py:151
  55.2 0.8 multiply_reduce_fusion.2
  56.0 0.8 copy.17
  56.9 1.9 %multiply_reduce_fusion.1 = (f32[512]{0:T(512)S(1)}, f32[512,128]{0,1:T(8,128)S(1)}) fusion(bf16[512,2048]{1,0:T(8,128)(2,1)S(1)} %bitcast.35, bf16[2048,128]{1,0:T(8,128)(2,1)} %param.14), kind=kOutput, calls=%fused_computation.29 | convolution fusion | flops 268566016 | bytes 2885632 | tf_op jit(solution)/shard_map/dot_general | solution.py:153
  58.8 0.8 copy.18
  59.6 13.1 %all-reduce = (f32[512]{0:T(512)S(1)}, f32[512]{0:T(512)S(1)}) all-reduce(f32[512]{0:T(512)S(1)} %get-tuple-element.12, f32[512]{0:T(512)S(1)} %get-tuple-element.14), channel_id=1, replica_groups=mesh['req'=64,'tp'=8] {'tp'}, use_global_device_ids=true, to_apply=%region_1.2 | all-reduce | flops 1024 | bytes 8192 | tf_op jit(solution)/shard_map/psum | solution.py:155
  72.7 1.1 multiply_bitcast_fusion.1
  73.9 1.1 multiply_bitcast_fusion
  74.9 1.3 fusion.16
  76.2 0.8 pad_maximum_fusion.2.nk_ref
  77.0 0.8 pad_maximum_fusion.1.q_ref
  77.8 1.4 %convolution_convert_fusion.nv_ref = bf16[512,128]{1,0:T(8,128)(2,1)} fusion(bf16[512,2048]{1,0:T(8,128)(2,1)S(1)} %bitcast.36, bf16[2048,128]{1,0:T(8,128)(2,1)S(1)} %copy-done.5), kind=kOutput, calls=%fused_computation.2 | convolution fusion | flops 268500992 | bytes 2752512 | tf_op jit(solution)/shard_map/dot_general | solution.py:154
  79.1 9.9 %all-to-all-done.1 = bf16[64,16,256]{2,1,0:T(8,128)(2,1)S(1)} async-done(((bf16[64,16,256]{2,1,0:T(8,128)(2,1)}), bf16[64,16,256]{2,1,0:T(8,128)(2,1)S(1)}, u32[]{:S(2)}, u32[]{:S(2)}) %all-to-all-start.1) | async-done | bytes 524320 | tf_op jit(solution)/shard_map/all_to_all | solution.py:151
  89.0 0.8 copy-done.2
  89.8 10.3 %shard_map.131 = bf16[512,2048]{1,0:T(8,128)(2,1)} custom-call(s32[1]{0:T(128)S(6)} %copy.23.len_ref, bf16[512,128]{1,0:T(8,128)(2,1)} %pad_maximum_fusion.1.q_ref, bf16[1024,256]{1,0:T(8,128)(2,1)} %bitcast.39, bf16[4096,256]{1,0:T(8,128)(2,1)} %bitcast.38, bf16[512,128]{1,0:T(8,128)(2,1)} %pad_maximum_fusion.2.nk_ref, ...), custom_call_target="tpu_custom_call" | custom-call | tf_op jit(solution)/shard_map/pallas_call | solution.py:110
  100.2 4.4 %all-to-all-start.2 = ((bf16[8,64,2048]{2,1,0:T(8,128)(2,1)}), bf16[8,64,2048]{2,1,0:T(8,128)(2,1)S(1)}, u32[]{:S(2)}, u32[]{:S(2)}) async-start(bf16[8,64,2048]{2,1,0:T(8,128)(2,1)} %bitcast.37), calls=%async_computation.2 | async-start | bytes 4194304 | tf_op jit(solution)/shard_map/all_to_all | solution.py:185
  104.8 0.8 copy.21
  105.7 30.0 %all-to-all-done.2 = bf16[8,64,2048]{2,1,0:T(8,128)(2,1)S(1)} async-done(((bf16[8,64,2048]{2,1,0:T(8,128)(2,1)}), bf16[8,64,2048]{2,1,0:T(8,128)(2,1)S(1)}, u32[]{:S(2)}, u32[]{:S(2)}) %all-to-all-start.2) | async-done | bytes 2097184 | tf_op jit(solution)/shard_map/all_to_all | solution.py:185
  136.2 0.9 fusion.2
  (30 shorter events, 0.8 us)
Async XLA Ops:
  0.6 54.5 %copy-start = (bf16[2048,128]{1,0:T(8,128)(2,1)S(1)}, bf16[2048,128]{1,0:T(8,128)(2,1)}, u32[]{:S(2)}) copy-start(bf16[2048,128]{1,0:T(8,128)(2,1)} %param.13) | copy-start | bytes 1572868
  3.3 6.0 %copy-start.9 = (s32[64]{0:T(128)S(1)}, s32[64]{0:T(128)}, u32[]{:S(2)}) copy-start(s32[64]{0:T(128)} %param.21) | copy-start | bytes 772
  3.3 6.0 %copy-start.1 = (bf16[8,16,256]{2,1,0:T(8,128)(2,1)S(1)}, bf16[8,16,256]{2,1,0:T(8,128)(2,1)}, u32[]{:S(2)}) copy-start(bf16[8,16,256]{2,1,0:T(8,128)(2,1)} %param.22) | copy-start | bytes 196612
  3.3 32.3 %all-to-all-start = ((bf16[8,64,2048]{2,1,0:T(8,128)(2,1)}), bf16[8,64,2048]{2,1,0:T(8,128)(2,1)S(1)}, u32[]{:S(2)}, u32[]{:S(2)}) async-start(bf16[8,64,2048]{2,1,0:T(8,128)(2,1)} %broadcast_in_dim.17), calls=%async_computation | async-start | bytes 4194304 | tf_op jit(solution)/shard_map/all_to_all | solution.py:147
  35.6 53.4 %all-to-all-start.1 = ((bf16[64,16,256]{2,1,0:T(8,128)(2,1)}), bf16[64,16,256]{2,1,0:T(8,128)(2,1)S(1)}, u32[]{:S(2)}, u32[]{:S(2)}) async-start(bf16[64,16,256]{2,1,0:T(8,128)(2,1)} %broadcast_select_fusion), calls=%async_computation.1 | async-start | bytes 1048576 | tf_op jit(solution)/shard_map/all_to_all | solution.py:151
  56.0 16.7 %copy-start.7 = (f32[128]{0:T(128)S(1)}, f32[128]{0:T(128)}, u32[]{:S(2)}) copy-start(f32[128]{0:T(128)} %param.17) | copy-start | bytes 1540
  56.9 17.0 %copy-start.8 = (f32[128]{0:T(128)S(1)}, f32[128]{0:T(128)}, u32[]{:S(2)}) copy-start(f32[128]{0:T(128)} %param.18) | copy-start | bytes 1540
  72.7 5.1 %copy-start.5 = (bf16[2048,128]{1,0:T(8,128)(2,1)S(1)}, bf16[2048,128]{1,0:T(8,128)(2,1)}, u32[]{:S(2)}) copy-start(bf16[2048,128]{1,0:T(8,128)(2,1)} %param.15) | copy-start | bytes 1572868
  89.0 0.8 copy-start.2
  100.2 4.4 %copy-start.3 = (bf16[512,128]{1,0:T(8,128)(2,1)S(1)}, bf16[512,128]{1,0:T(8,128)(2,1)}, u32[]{:S(2)}) copy-start(bf16[512,128]{1,0:T(8,128)(2,1)} %convolution_convert_fusion.nv_ref) | copy-start | bytes 393220
  100.2 35.5 %all-to-all-start.2 = ((bf16[8,64,2048]{2,1,0:T(8,128)(2,1)}), bf16[8,64,2048]{2,1,0:T(8,128)(2,1)S(1)}, u32[]{:S(2)}, u32[]{:S(2)}) async-start(bf16[8,64,2048]{2,1,0:T(8,128)(2,1)} %bitcast.37), calls=%async_computation.2 | async-start | bytes 4194304 | tf_op jit(solution)/shard_map/all_to_all | solution.py:185
  104.7 31.5 %copy-start.4 = (bf16[1,64,2048]{2,1,0:T(8,128)(2,1)S(1)}, bf16[1,64,2048]{2,1,0:T(8,128)(2,1)}, u32[]{:S(2)}) copy-start(bf16[1,64,2048]{2,1,0:T(8,128)(2,1)} %param.12) | copy-start | bytes 786436
  104.7 31.5 %copy-start.6 = (f32[2048]{0:T(1024)S(1)}, f32[2048]{0:T(1024)}, u32[]{:S(2)}) copy-start(f32[2048]{0:T(1024)} %param.19) | copy-start | bytes 24580

commit v8 on v7

--- a/solution.py
+++ b/solution.py
@@ -80,7 +80,15 @@
             preferred_element_type=jnp.float32,
         ) * scale
         visible = visible_of(chunk)
-        if visible is not None:
+        if visible is not None and prefix_chunks < chunk < prefix_chunks + cache_chunks:
+            end = (chunk - prefix_chunks + 1) * KEY_BLOCK
+            part = lax.cond(
+                end <= length,
+                lambda p: p,
+                lambda p: jnp.where(visible, p, -1e30),
+                part,
+            )
+        elif visible is not None:
             part = jnp.where(visible, part, -1e30)
         score_ref[:, pl.ds(chunk * KEY_BLOCK, KEY_BLOCK)] = part
         peak = jnp.max(part, -1, keepdims=True)
@@ -89,9 +97,6 @@
     weighted = jnp.zeros((QUERY_BLOCK, HD), jnp.float32)
     for chunk in range(chunks):
         weights = jnp.exp(score_ref[:, pl.ds(chunk * KEY_BLOCK, KEY_BLOCK)] - row_peak)
-        visible = visible_of(chunk)
-        if visible is not None:
-            weights = jnp.where(visible, weights, 0.0)
         denominator = denominator + jnp.sum(weights, -1, keepdims=True)
         weighted = weighted + jnp.dot(
             weights.astype(jnp.bfloat16), values_of(chunk), preferred_element_type=jnp.float32

time: 138 us -> 142 us (1.029)
  the two profiles are of different devices: /device:TPU:39 before, /device:TPU:38 now
where the time goes in v8:
time: 142 us
  waiting for transfers between devices  61.5 us (43%)
  starting transfers between devices  28.9 us (20%)
  blocking collectives  15.7 us (11%)
  Pallas kernels  15.5 us (11%)
  other arithmetic  7.49 us (5%)
  local copies, waits for them, and re-layouts  6.72 us (5%)
  matrix products  4.11 us (3%)
  between operations  1.47 us (1%)
    all_to_all x1, waiting for transfers between devices, layer(): lax.all_to_all(blocks_out, 'tp', 0, 0, tiled=True).astype(jnp.float32)  30.3 us
    all_to_all x1, waiting for transfers between devices, layer(): lax.all_to_all(jnp.broadcast_to(tokens, (tp_size,) + tokens.shape[1:]), '...  25.3 us
    all_to_all x1, starting transfers between devices, layer(): chosen = lax.all_to_all(outgoing, 'req', 0, 0, tiled=True)  18.1 us
    psum x1, blocking collectives, layer(): lax.psum((jnp.sum(queries * queries, -1), jnp.sum(keys_new * keys_new, -1...  15.7 us
    pallas_call x1, Pallas kernels, attend(): pl.pallas_call(attend_kernel, grid_spec=pltpu.PrefetchScalarGridSpec(num_...  15.5 us
    all_to_all x1, starting transfers between devices, layer(): lax.all_to_all(jnp.broadcast_to(tokens, (tp_size,) + tokens.shape[1:]), '...  5.92 us
    all_to_all x1, waiting for transfers between devices, layer(): chosen = lax.all_to_all(outgoing, 'req', 0, 0, tiled=True)  5.89 us
    all_to_all x1, starting transfers between devices, layer(): lax.all_to_all(blocks_out, 'tp', 0, 0, tiled=True).astype(jnp.float32)  4.94 us
  transfers between devices with their start and end apart: 3, of which 3 were waited for; matrix products, arithmetic and copies ran while one was open for 10% of the time, Pallas kernels for 0%

profile of v8, /device:TPU:38, one launch (start us, length us, event | category | flops | bytes accessed | tf_op | source)
XLA Modules:
  0.0 141.5 jit_solution(7793684857269060926)
XLA Ops:
  0.6 2.6 %broadcast_in_dim.17 = bf16[8,64,2048]{2,1,0:T(8,128)(2,1)} broadcast(bf16[64,2048]{1,0:T(8,128)(2,1)} %bitcast.45), dimensions={1,2} | broadcast | bytes 2359296 | tf_op jit(solution)/shard_map/broadcast_in_dim | solution.py:153
  3.3 5.9 %all-to-all-start = ((bf16[8,64,2048]{2,1,0:T(8,128)(2,1)}), bf16[8,64,2048]{2,1,0:T(8,128)(2,1)S(1)}, u32[]{:S(2)}, u32[]{:S(2)}) async-start(bf16[8,64,2048]{2,1,0:T(8,128)(2,1)} %broadcast_in_dim.17), calls=%async_computation | async-start | bytes 4194304 | tf_op jit(solution)/shard_map/all_to_all | solution.py:152
  9.9 0.6 gather_fusion
  10.5 0.9 broadcast_select_fusion
  11.5 25.3 %all-to-all-done = bf16[8,64,2048]{2,1,0:T(8,128)(2,1)S(1)} async-done(((bf16[8,64,2048]{2,1,0:T(8,128)(2,1)}), bf16[8,64,2048]{2,1,0:T(8,128)(2,1)S(1)}, u32[]{:S(2)}, u32[]{:S(2)}) %all-to-all-start) | async-done | bytes 2097184 | tf_op jit(solution)/shard_map/all_to_all | solution.py:152
  36.8 18.1 %all-to-all-start.1 = ((bf16[64,16,256]{2,1,0:T(8,128)(2,1)}), bf16[64,16,256]{2,1,0:T(8,128)(2,1)S(1)}, u32[]{:S(2)}, u32[]{:S(2)}) async-start(bf16[64,16,256]{2,1,0:T(8,128)(2,1)} %broadcast_select_fusion), calls=%async_computation.1 | async-start | bytes 1048576 | tf_op jit(solution)/shard_map/all_to_all | solution.py:156
  54.9 0.8 multiply_reduce_fusion.2
  55.7 0.8 copy.17
  56.6 1.9 %multiply_reduce_fusion.1 = (f32[512]{0:T(512)S(1)}, f32[512,128]{0,1:T(8,128)S(1)}) fusion(bf16[512,2048]{1,0:T(8,128)(2,1)S(1)} %bitcast.35, bf16[2048,128]{1,0:T(8,128)(2,1)} %param.14), kind=kOutput, calls=%fused_computation.29 | convolution fusion | flops 268566016 | bytes 2885632 | tf_op jit(solution)/shard_map/dot_general | solution.py:158
  58.5 0.8 copy.18
  59.3 15.7 %all-reduce = (f32[512]{0:T(512)S(1)}, f32[512]{0:T(512)S(1)}) all-reduce(f32[512]{0:T(512)S(1)} %get-tuple-element.12, f32[512]{0:T(512)S(1)} %get-tuple-element.14), channel_id=1, replica_groups=mesh['req'=64,'tp'=8] {'tp'}, use_global_device_ids=true, to_apply=%region_1.2 | all-reduce | flops 1024 | bytes 8192 | tf_op jit(solution)/shard_map/psum | solution.py:160
  75.0 1.1 multiply_bitcast_fusion.1
  76.2 1.1 multiply_bitcast_fusion
  77.3 1.3 fusion.16
  78.6 0.8 pad_maximum_fusion.2.nk_ref
  79.3 0.8 pad_maximum_fusion.1.q_ref
  80.1 1.4 convolution_convert_fusion.nv_ref
  81.5 5.9 %all-to-all-done.1 = bf16[64,16,256]{2,1,0:T(8,128)(2,1)S(1)} async-done(((bf16[64,16,256]{2,1,0:T(8,128)(2,1)}), bf16[64,16,256]{2,1,0:T(8,128)(2,1)S(1)}, u32[]{:S(2)}, u32[]{:S(2)}) %all-to-all-start.1) | async-done | bytes 524320 | tf_op jit(solution)/shard_map/all_to_all | solution.py:156
  87.4 0.8 copy-done.2
  88.2 15.5 %shard_map.131 = bf16[512,2048]{1,0:T(8,128)(2,1)} custom-call(s32[1]{0:T(128)S(6)} %copy.23.len_ref, bf16[512,128]{1,0:T(8,128)(2,1)} %pad_maximum_fusion.1.q_ref, bf16[1024,256]{1,0:T(8,128)(2,1)} %bitcast.39, bf16[4096,256]{1,0:T(8,128)(2,1)} %bitcast.38, bf16[512,128]{1,0:T(8,128)(2,1)} %pad_maximum_fusion.2.nk_ref, ...), custom_call_target="tpu_custom_call" | custom-call | tf_op jit(solution)/shard_map/pallas_call | solution.py:115
  103.7 4.9 %all-to-all-start.2 = ((bf16[8,64,2048]{2,1,0:T(8,128)(2,1)}), bf16[8,64,2048]{2,1,0:T(8,128)(2,1)S(1)}, u32[]{:S(2)}, u32[]{:S(2)}) async-start(bf16[8,64,2048]{2,1,0:T(8,128)(2,1)} %bitcast.37), calls=%async_computation.2 | async-start | bytes 4194304 | tf_op jit(solution)/shard_map/all_to_all | solution.py:190
  109.0 0.8 copy.21
  109.8 30.3 %all-to-all-done.2 = bf16[8,64,2048]{2,1,0:T(8,128)(2,1)S(1)} async-done(((bf16[8,64,2048]{2,1,0:T(8,128)(2,1)}), bf16[8,64,2048]{2,1,0:T(8,128)(2,1)S(1)}, u32[]{:S(2)}, u32[]{:S(2)}) %all-to-all-start.2) | async-done | bytes 2097184 | tf_op jit(solution)/shard_map/all_to_all | solution.py:190
  140.7 0.9 fusion.2
  (30 shorter events, 0.8 us)
Async XLA Ops:
  0.6 54.2 %copy-start = (bf16[2048,128]{1,0:T(8,128)(2,1)S(1)}, bf16[2048,128]{1,0:T(8,128)(2,1)}, u32[]{:S(2)}) copy-start(bf16[2048,128]{1,0:T(8,128)(2,1)} %param.13) | copy-start | bytes 1572868
  3.3 6.6 %copy-start.9 = (s32[64]{0:T(128)S(1)}, s32[64]{0:T(128)}, u32[]{:S(2)}) copy-start(s32[64]{0:T(128)} %param.21) | copy-start | bytes 772
  3.3 6.6 %copy-start.1 = (bf16[8,16,256]{2,1,0:T(8,128)(2,1)S(1)}, bf16[8,16,256]{2,1,0:T(8,128)(2,1)}, u32[]{:S(2)}) copy-start(bf16[8,16,256]{2,1,0:T(8,128)(2,1)} %param.22) | copy-start | bytes 196612
  3.3 33.5 %all-to-all-start = ((bf16[8,64,2048]{2,1,0:T(8,128)(2,1)}), bf16[8,64,2048]{2,1,0:T(8,128)(2,1)S(1)}, u32[]{:S(2)}, u32[]{:S(2)}) async-start(bf16[8,64,2048]{2,1,0:T(8,128)(2,1)} %broadcast_in_dim.17), calls=%async_computation | async-start | bytes 4194304 | tf_op jit(solution)/shard_map/all_to_all | solution.py:152
  36.8 50.6 %all-to-all-start.1 = ((bf16[64,16,256]{2,1,0:T(8,128)(2,1)}), bf16[64,16,256]{2,1,0:T(8,128)(2,1)S(1)}, u32[]{:S(2)}, u32[]{:S(2)}) async-start(bf16[64,16,256]{2,1,0:T(8,128)(2,1)} %broadcast_select_fusion), calls=%async_computation.1 | async-start | bytes 1048576 | tf_op jit(solution)/shard_map/all_to_all | solution.py:156
  55.7 19.3 %copy-start.7 = (f32[128]{0:T(128)S(1)}, f32[128]{0:T(128)}, u32[]{:S(2)}) copy-start(f32[128]{0:T(128)} %param.17) | copy-start | bytes 1540
  56.6 19.6 %copy-start.8 = (f32[128]{0:T(128)S(1)}, f32[128]{0:T(128)}, u32[]{:S(2)}) copy-start(f32[128]{0:T(128)} %param.18) | copy-start | bytes 1540
  75.0 5.1 %copy-start.5 = (bf16[2048,128]{1,0:T(8,128)(2,1)S(1)}, bf16[2048,128]{1,0:T(8,128)(2,1)}, u32[]{:S(2)}) copy-start(bf16[2048,128]{1,0:T(8,128)(2,1)} %param.15) | copy-start | bytes 1572868
  87.4 0.8 copy-start.2
  103.7 4.9 %copy-start.3 = (bf16[512,128]{1,0:T(8,128)(2,1)S(1)}, bf16[512,128]{1,0:T(8,128)(2,1)}, u32[]{:S(2)}) copy-start(bf16[512,128]{1,0:T(8,128)(2,1)} %convolution_convert_fusion.nv_ref) | copy-start | bytes 393220
  103.7 36.4 %all-to-all-start.2 = ((bf16[8,64,2048]{2,1,0:T(8,128)(2,1)}), bf16[8,64,2048]{2,1,0:T(8,128)(2,1)S(1)}, u32[]{:S(2)}, u32[]{:S(2)}) async-start(bf16[8,64,2048]{2,1,0:T(8,128)(2,1)} %bitcast.37), calls=%async_computation.2 | async-start | bytes 4194304 | tf_op jit(solution)/shard_map/all_to_all | solution.py:190
  108.8 31.9 %copy-start.4 = (bf16[1,64,2048]{2,1,0:T(8,128)(2,1)S(1)}, bf16[1,64,2048]{2,1,0:T(8,128)(2,1)}, u32[]{:S(2)}) copy-start(bf16[1,64,2048]{2,1,0:T(8,128)(2,1)} %param.12) | copy-start | bytes 786436
  108.8 31.9 %copy-start.6 = (f32[2048]{0:T(1024)S(1)}, f32[2048]{0:T(1024)}, u32[]{:S(2)}) copy-start(f32[2048]{0:T(1024)} %param.19) | copy-start | bytes 24580

commit v9 on v7

--- a/solution.py
+++ b/solution.py
@@ -33,7 +33,7 @@
     return values_in * lax.rsqrt(mean_sq + 1e-06) * gain_vector
 
 
-QUERY_BLOCK = 128
+QUERY_BLOCK = 256
 KEY_BLOCK = 512
 
 
@@ -89,9 +89,6 @@
     weighted = jnp.zeros((QUERY_BLOCK, HD), jnp.float32)
     for chunk in range(chunks):
         weights = jnp.exp(score_ref[:, pl.ds(chunk * KEY_BLOCK, KEY_BLOCK)] - row_peak)
-        visible = visible_of(chunk)
-        if visible is not None:
-            weights = jnp.where(visible, weights, 0.0)
         denominator = denominator + jnp.sum(weights, -1, keepdims=True)
         weighted = weighted + jnp.dot(
             weights.astype(jnp.bfloat16), values_of(chunk), preferred_element_type=jnp.float32

time: 138 us -> 136 us (0.986)
  no operation moved by 1% of the time
where the time goes in v9:
time: 136 us
  waiting for transfers between devices  64.5 us (47%)
  starting transfers between devices  29.3 us (22%)
  blocking collectives  13.1 us (10%)
  Pallas kernels  9.08 us (7%)
  other arithmetic  7.49 us (6%)
  local copies, waits for them, and re-layouts  6.72 us (5%)
  matrix products  4.1 us (3%)
  between operations  1.47 us (1%)
    all_to_all x1, waiting for transfers between devices, layer(): lax.all_to_all(blocks_out, 'tp', 0, 0, tiled=True).astype(jnp.float32)  30 us
    all_to_all x1, waiting for transfers between devices, layer(): lax.all_to_all(jnp.broadcast_to(tokens, (tp_size,) + tokens.shape[1:]), '...  24.7 us
    all_to_all x1, starting transfers between devices, layer(): chosen = lax.all_to_all(outgoing, 'req', 0, 0, tiled=True)  19.6 us
    psum x1, blocking collectives, layer(): lax.psum((jnp.sum(queries * queries, -1), jnp.sum(keys_new * keys_new, -1...  13.1 us
    all_to_all x1, waiting for transfers between devices, layer(): chosen = lax.all_to_all(outgoing, 'req', 0, 0, tiled=True)  9.87 us
    pallas_call x1, Pallas kernels, attend(): pl.pallas_call(attend_kernel, grid_spec=pltpu.PrefetchScalarGridSpec(num_...  9.08 us
    all_to_all x1, starting transfers between devices, layer(): lax.all_to_all(jnp.broadcast_to(tokens, (tp_size,) + tokens.shape[1:]), '...  5.36 us
    all_to_all x1, starting transfers between devices, layer(): lax.all_to_all(blocks_out, 'tp', 0, 0, tiled=True).astype(jnp.float32)  4.38 us
  transfers between devices with their start and end apart: 3, of which 3 were waited for; matrix products, arithmetic and copies ran while one was open for 10% of the time, Pallas kernels for 0%

profile of v9, /device:TPU:39, one launch (start us, length us, event | category | flops | bytes accessed | tf_op | source)
XLA Modules:
  0.0 135.8 jit_solution(9200014229562747968)
XLA Ops:
  0.6 2.6 %broadcast_in_dim.17 = bf16[8,64,2048]{2,1,0:T(8,128)(2,1)} broadcast(bf16[64,2048]{1,0:T(8,128)(2,1)} %bitcast.45), dimensions={1,2} | broadcast | bytes 2359296 | tf_op jit(solution)/shard_map/broadcast_in_dim | solution.py:145
  3.3 5.4 %all-to-all-start = ((bf16[8,64,2048]{2,1,0:T(8,128)(2,1)}), bf16[8,64,2048]{2,1,0:T(8,128)(2,1)S(1)}, u32[]{:S(2)}, u32[]{:S(2)}) async-start(bf16[8,64,2048]{2,1,0:T(8,128)(2,1)} %broadcast_in_dim.17), calls=%async_computation | async-start | bytes 4194304 | tf_op jit(solution)/shard_map/all_to_all | solution.py:144
  9.3 0.6 gather_fusion
  10.0 0.9 broadcast_select_fusion
  10.9 24.7 %all-to-all-done = bf16[8,64,2048]{2,1,0:T(8,128)(2,1)S(1)} async-done(((bf16[8,64,2048]{2,1,0:T(8,128)(2,1)}), bf16[8,64,2048]{2,1,0:T(8,128)(2,1)S(1)}, u32[]{:S(2)}, u32[]{:S(2)}) %all-to-all-start) | async-done | bytes 2097184 | tf_op jit(solution)/shard_map/all_to_all | solution.py:144
  35.6 19.6 %all-to-all-start.1 = ((bf16[64,16,256]{2,1,0:T(8,128)(2,1)}), bf16[64,16,256]{2,1,0:T(8,128)(2,1)S(1)}, u32[]{:S(2)}, u32[]{:S(2)}) async-start(bf16[64,16,256]{2,1,0:T(8,128)(2,1)} %broadcast_select_fusion), calls=%async_computation.1 | async-start | bytes 1048576 | tf_op jit(solution)/shard_map/all_to_all | solution.py:148
  55.2 0.8 multiply_reduce_fusion.2
  56.0 0.8 copy.17
  56.9 1.9 %multiply_reduce_fusion.1 = (f32[512]{0:T(512)S(1)}, f32[512,128]{0,1:T(8,128)S(1)}) fusion(bf16[512,2048]{1,0:T(8,128)(2,1)S(1)} %bitcast.35, bf16[2048,128]{1,0:T(8,128)(2,1)} %param.14), kind=kOutput, calls=%fused_computation.29 | convolution fusion | flops 268566016 | bytes 2885632 | tf_op jit(solution)/shard_map/dot_general | solution.py:150
  58.8 0.8 copy.18
  59.6 13.1 %all-reduce = (f32[512]{0:T(512)S(1)}, f32[512]{0:T(512)S(1)}) all-reduce(f32[512]{0:T(512)S(1)} %get-tuple-element.12, f32[512]{0:T(512)S(1)} %get-tuple-element.14), channel_id=1, replica_groups=mesh['req'=64,'tp'=8] {'tp'}, use_global_device_ids=true, to_apply=%region_1.2 | all-reduce | flops 1024 | bytes 8192 | tf_op jit(solution)/shard_map/psum | solution.py:152
  72.7 1.1 multiply_bitcast_fusion.1
  73.9 1.1 multiply_bitcast_fusion
  74.9 1.3 fusion.16
  76.2 0.8 pad_maximum_fusion.2.nk_ref
  77.0 0.8 pad_maximum_fusion.1.q_ref
  77.8 1.4 %convolution_convert_fusion.nv_ref = bf16[512,128]{1,0:T(8,128)(2,1)} fusion(bf16[512,2048]{1,0:T(8,128)(2,1)S(1)} %bitcast.36, bf16[2048,128]{1,0:T(8,128)(2,1)S(1)} %copy-done.5), kind=kOutput, calls=%fused_computation.2 | convolution fusion | flops 268500992 | bytes 2752512 | tf_op jit(solution)/shard_map/dot_general | solution.py:151
  79.1 9.9 %all-to-all-done.1 = bf16[64,16,256]{2,1,0:T(8,128)(2,1)S(1)} async-done(((bf16[64,16,256]{2,1,0:T(8,128)(2,1)}), bf16[64,16,256]{2,1,0:T(8,128)(2,1)S(1)}, u32[]{:S(2)}, u32[]{:S(2)}) %all-to-all-start.1) | async-done | bytes 524320 | tf_op jit(solution)/shard_map/all_to_all | solution.py:148
  89.0 0.8 copy-done.2
  89.8 9.1 %shard_map.131 = bf16[512,2048]{1,0:T(8,128)(2,1)} custom-call(s32[1]{0:T(128)S(6)} %copy.23.len_ref, bf16[512,128]{1,0:T(8,128)(2,1)} %pad_maximum_fusion.1.q_ref, bf16[1024,256]{1,0:T(8,128)(2,1)} %bitcast.39, bf16[4096,256]{1,0:T(8,128)(2,1)} %bitcast.38, bf16[512,128]{1,0:T(8,128)(2,1)} %pad_maximum_fusion.2.nk_ref, ...), custom_call_target="tpu_custom_call" | custom-call | tf_op jit(solution)/shard_map/pallas_call | solution.py:107
  98.9 4.4 %all-to-all-start.2 = ((bf16[8,64,2048]{2,1,0:T(8,128)(2,1)}), bf16[8,64,2048]{2,1,0:T(8,128)(2,1)S(1)}, u32[]{:S(2)}, u32[]{:S(2)}) async-start(bf16[8,64,2048]{2,1,0:T(8,128)(2,1)} %bitcast.37), calls=%async_computation.2 | async-start | bytes 4194304 | tf_op jit(solution)/shard_map/all_to_all | solution.py:182
  103.6 0.8 copy.21
  104.4 30.0 %all-to-all-done.2 = bf16[8,64,2048]{2,1,0:T(8,128)(2,1)S(1)} async-done(((bf16[8,64,2048]{2,1,0:T(8,128)(2,1)}), bf16[8,64,2048]{2,1,0:T(8,128)(2,1)S(1)}, u32[]{:S(2)}, u32[]{:S(2)}) %all-to-all-start.2) | async-done | bytes 2097184 | tf_op jit(solution)/shard_map/all_to_all | solution.py:182
  134.9 0.9 fusion.2
  (30 shorter events, 0.8 us)
Async XLA Ops:
  0.6 54.5 %copy-start = (bf16[2048,128]{1,0:T(8,128)(2,1)S(1)}, bf16[2048,128]{1,0:T(8,128)(2,1)}, u32[]{:S(2)}) copy-start(bf16[2048,128]{1,0:T(8,128)(2,1)} %param.13) | copy-start | bytes 1572868
  3.3 6.0 %copy-start.9 = (s32[64]{0:T(128)S(1)}, s32[64]{0:T(128)}, u32[]{:S(2)}) copy-start(s32[64]{0:T(128)} %param.21) | copy-start | bytes 772
  3.3 6.0 %copy-start.1 = (bf16[8,16,256]{2,1,0:T(8,128)(2,1)S(1)}, bf16[8,16,256]{2,1,0:T(8,128)(2,1)}, u32[]{:S(2)}) copy-start(bf16[8,16,256]{2,1,0:T(8,128)(2,1)} %param.22) | copy-start | bytes 196612
  3.3 32.3 %all-to-all-start = ((bf16[8,64,2048]{2,1,0:T(8,128)(2,1)}), bf16[8,64,2048]{2,1,0:T(8,128)(2,1)S(1)}, u32[]{:S(2)}, u32[]{:S(2)}) async-start(bf16[8,64,2048]{2,1,0:T(8,128)(2,1)} %broadcast_in_dim.17), calls=%async_computation | async-start | bytes 4194304 | tf_op jit(solution)/shard_map/all_to_all | solution.py:144
  35.6 53.4 %all-to-all-start.1 = ((bf16[64,16,256]{2,1,0:T(8,128)(2,1)}), bf16[64,16,256]{2,1,0:T(8,128)(2,1)S(1)}, u32[]{:S(2)}, u32[]{:S(2)}) async-start(bf16[64,16,256]{2,1,0:T(8,128)(2,1)} %broadcast_select_fusion), calls=%async_computation.1 | async-start | bytes 1048576 | tf_op jit(solution)/shard_map/all_to_all | solution.py:148
  56.0 16.7 %copy-start.7 = (f32[128]{0:T(128)S(1)}, f32[128]{0:T(128)}, u32[]{:S(2)}) copy-start(f32[128]{0:T(128)} %param.17) | copy-start | bytes 1540
  56.9 17.0 %copy-start.8 = (f32[128]{0:T(128)S(1)}, f32[128]{0:T(128)}, u32[]{:S(2)}) copy-start(f32[128]{0:T(128)} %param.18) | copy-start | bytes 1540
  72.7 5.1 %copy-start.5 = (bf16[2048,128]{1,0:T(8,128)(2,1)S(1)}, bf16[2048,128]{1,0:T(8,128)(2,1)}, u32[]{:S(2)}) copy-start(bf16[2048,128]{1,0:T(8,128)(2,1)} %param.15) | copy-start | bytes 1572868
  89.0 0.8 copy-start.2
  98.9 4.4 %copy-start.3 = (bf16[512,128]{1,0:T(8,128)(2,1)S(1)}, bf16[512,128]{1,0:T(8,128)(2,1)}, u32[]{:S(2)}) copy-start(bf16[512,128]{1,0:T(8,128)(2,1)} %convolution_convert_fusion.nv_ref) | copy-start | bytes 393220
  98.9 35.5 %all-to-all-start.2 = ((bf16[8,64,2048]{2,1,0:T(8,128)(2,1)}), bf16[8,64,2048]{2,1,0:T(8,128)(2,1)S(1)}, u32[]{:S(2)}, u32[]{:S(2)}) async-start(bf16[8,64,2048]{2,1,0:T(8,128)(2,1)} %bitcast.37), calls=%async_computation.2 | async-start | bytes 4194304 | tf_op jit(solution)/shard_map/all_to_all | solution.py:182
  103.4 31.5 %copy-start.4 = (bf16[1,64,2048]{2,1,0:T(8,128)(2,1)S(1)}, bf16[1,64,2048]{2,1,0:T(8,128)(2,1)}, u32[]{:S(2)}) copy-start(bf16[1,64,2048]{2,1,0:T(8,128)(2,1)} %param.12) | copy-start | bytes 786436
  103.4 31.5 %copy-start.6 = (f32[2048]{0:T(1024)S(1)}, f32[2048]{0:T(1024)}, u32[]{:S(2)}) copy-start(f32[2048]{0:T(1024)} %param.19) | copy-start | bytes 24580

commit v10 on v9

--- a/solution.py
+++ b/solution.py
@@ -125,6 +125,27 @@
     )(cache_lens, queries, prefix_pairs, cache_pairs, keys_new, values_new, w_out)
 
 
+def repeat_kernel(in_ref, out_ref, sems):
+    copies = [
+        pltpu.make_async_copy(in_ref, out_ref.at[pl.ds(i, 1)], sems.at[i])
+        for i in range(out_ref.shape[0])
+    ]
+    for copy in copies:
+        copy.start()
+    for copy in copies:
+        copy.wait()
+
+
+def repeat_rows(block, copies):
+    return pl.pallas_call(
+        repeat_kernel,
+        in_specs=[pl.BlockSpec(memory_space=pltpu.VMEM)],
+        out_specs=pl.BlockSpec(memory_space=pl.ANY),
+        out_shape=jax.ShapeDtypeStruct((copies,) + block.shape[1:], block.dtype),
+        scratch_shapes=[pltpu.SemaphoreType.DMA((copies,))],
+    )(block)
+
+
 def layer(
     tokens,
     w_q,
@@ -142,7 +163,7 @@
     heads_local = w_q.shape[1] // HD
     tp_size = lax.axis_size("tp")
     flat_rows = lax.all_to_all(
-        jnp.broadcast_to(tokens, (tp_size,) + tokens.shape[1:]), "tp", 0, 0, tiled=True
+        repeat_rows(tokens, tp_size), "tp", 0, 0, tiled=True
     ).reshape(-1, tokens.shape[2])
     outgoing = jnp.take(prefix_cache, group_ids, axis=0)
     chosen = lax.all_to_all(outgoing, "req", 0, 0, tiled=True)

time: 136 us -> 136 us (level)
  local copies, waits for them, and re-layouts: 6.72 us -> 4.11 us
  Pallas kernels: 9.08 us -> 11.5 us
    broadcast_in_dim x1 -> x0, local copies, waits for them, and re-layouts: 2.62 us -> none  [layer(): jnp.broadcast_to(tokens, (tp_size,) + tokens.shape[1:])]
    pallas_call x0 -> x1, Pallas kernels: none -> 2.43 us  [repeat_rows(): pl.pallas_call(repeat_kernel, in_specs=[pl.BlockSpec(memory_space=pltpu.V...]
where the time goes in v10:
time: 136 us
  waiting for transfers between devices  64.5 us (47%)
  starting transfers between devices  29.3 us (22%)
  blocking collectives  13.1 us (10%)
  Pallas kernels  11.5 us (8%)
  other arithmetic  7.49 us (6%)
  local copies, waits for them, and re-layouts  4.11 us (3%)
  matrix products  4.11 us (3%)
  between operations  1.49 us (1%)
    all_to_all x1, waiting for transfers between devices, layer(): lax.all_to_all(blocks_out, 'tp', 0, 0, tiled=True).astype(jnp.float32)  30 us
    all_to_all x1, waiting for transfers between devices, layer(): lax.all_to_all(repeat_rows(tokens, tp_size), 'tp', 0, 0, tiled=True)  24.7 us
    all_to_all x1, starting transfers between devices, layer(): chosen = lax.all_to_all(outgoing, 'req', 0, 0, tiled=True)  19.6 us
    psum x1, blocking collectives, layer(): lax.psum((jnp.sum(queries * queries, -1), jnp.sum(keys_new * keys_new, -1...  13.1 us
    all_to_all x1, waiting for transfers between devices, layer(): chosen = lax.all_to_all(outgoing, 'req', 0, 0, tiled=True)  9.87 us
    pallas_call x1, Pallas kernels, attend(): pl.pallas_call(attend_kernel, grid_spec=pltpu.PrefetchScalarGridSpec(num_...  9.08 us
    all_to_all x1, starting transfers between devices, layer(): lax.all_to_all(repeat_rows(tokens, tp_size), 'tp', 0, 0, tiled=True)  5.37 us
    all_to_all x1, starting transfers between devices, layer(): lax.all_to_all(blocks_out, 'tp', 0, 0, tiled=True).astype(jnp.float32)  4.38 us
  transfers between devices with their start and end apart: 3, of which 3 were waited for; matrix products, arithmetic and copies ran while one was open for 10% of the time, Pallas kernels for 0%

profile of v10, /device:TPU:39, one launch (start us, length us, event | category | flops | bytes accessed | tf_op | source)
XLA Modules:
  0.0 135.6 jit_solution(17091865074842868887)
XLA Ops:
  0.6 2.4 %shard_map.131 = bf16[8,64,2048]{2,1,0:T(8,128)(2,1)} custom-call(bf16[1,64,2048]{2,1,0:T(8,128)(2,1)} %in_ref.1), custom_call_target="tpu_custom_call" | custom-call | tf_op jit(solution)/shard_map/pallas_call | solution.py:140
  3.1 5.4 %all-to-all-start = ((bf16[8,64,2048]{2,1,0:T(8,128)(2,1)}), bf16[8,64,2048]{2,1,0:T(8,128)(2,1)S(1)}, u32[]{:S(2)}, u32[]{:S(2)}) async-start(bf16[8,64,2048]{2,1,0:T(8,128)(2,1)} %shard_map.131), calls=%async_computation | async-start | bytes 4194304 | tf_op jit(solution)/shard_map/all_to_all | solution.py:165
  9.2 0.6 gather_fusion
  9.8 0.9 broadcast_select_fusion
  10.8 24.7 %all-to-all-done = bf16[8,64,2048]{2,1,0:T(8,128)(2,1)S(1)} async-done(((bf16[8,64,2048]{2,1,0:T(8,128)(2,1)}), bf16[8,64,2048]{2,1,0:T(8,128)(2,1)S(1)}, u32[]{:S(2)}, u32[]{:S(2)}) %all-to-all-start) | async-done | bytes 2097184 | tf_op jit(solution)/shard_map/all_to_all | solution.py:165
  35.4 19.6 %all-to-all-start.1 = ((bf16[64,16,256]{2,1,0:T(8,128)(2,1)}), bf16[64,16,256]{2,1,0:T(8,128)(2,1)S(1)}, u32[]{:S(2)}, u32[]{:S(2)}) async-start(bf16[64,16,256]{2,1,0:T(8,128)(2,1)} %broadcast_select_fusion), calls=%async_computation.1 | async-start | bytes 1048576 | tf_op jit(solution)/shard_map/all_to_all | solution.py:169
  55.0 0.8 multiply_reduce_fusion.2
  55.9 0.8 copy.17
  56.7 1.9 %multiply_reduce_fusion.1 = (f32[512]{0:T(512)S(1)}, f32[512,128]{0,1:T(8,128)S(1)}) fusion(bf16[512,2048]{1,0:T(8,128)(2,1)S(1)} %bitcast.34, bf16[2048,128]{1,0:T(8,128)(2,1)} %param.14), kind=kOutput, calls=%fused_computation.29 | convolution fusion | flops 268566016 | bytes 2885632 | tf_op jit(solution)/shard_map/dot_general | solution.py:171
  58.6 0.8 copy.18
  59.4 13.1 %all-reduce = (f32[512]{0:T(512)S(1)}, f32[512]{0:T(512)S(1)}) all-reduce(f32[512]{0:T(512)S(1)} %get-tuple-element.12, f32[512]{0:T(512)S(1)} %get-tuple-element.14), channel_id=1, replica_groups=mesh['req'=64,'tp'=8] {'tp'}, use_global_device_ids=true, to_apply=%region_1.2 | all-reduce | flops 1024 | bytes 8192 | tf_op jit(solution)/shard_map/psum | solution.py:173
  72.6 1.1 multiply_bitcast_fusion.1
  73.7 1.1 multiply_bitcast_fusion
  74.8 1.3 fusion.16
  76.1 0.8 pad_maximum_fusion.2.nk_ref
  76.9 0.8 pad_maximum_fusion.1.q_ref
  77.6 1.4 %convolution_convert_fusion.nv_ref = bf16[512,128]{1,0:T(8,128)(2,1)} fusion(bf16[512,2048]{1,0:T(8,128)(2,1)S(1)} %bitcast.35, bf16[2048,128]{1,0:T(8,128)(2,1)S(1)} %copy-done.5), kind=kOutput, calls=%fused_computation.2 | convolution fusion | flops 268500992 | bytes 2752512 | tf_op jit(solution)/shard_map/dot_general | solution.py:172
  79.0 9.9 %all-to-all-done.1 = bf16[64,16,256]{2,1,0:T(8,128)(2,1)S(1)} async-done(((bf16[64,16,256]{2,1,0:T(8,128)(2,1)}), bf16[64,16,256]{2,1,0:T(8,128)(2,1)S(1)}, u32[]{:S(2)}, u32[]{:S(2)}) %all-to-all-start.1) | async-done | bytes 524320 | tf_op jit(solution)/shard_map/all_to_all | solution.py:169
  88.9 0.8 copy-done.2
  89.7 9.1 %shard_map.132 = bf16[512,2048]{1,0:T(8,128)(2,1)} custom-call(s32[1]{0:T(128)S(6)} %copy.23.len_ref, bf16[512,128]{1,0:T(8,128)(2,1)} %pad_maximum_fusion.1.q_ref, bf16[1024,256]{1,0:T(8,128)(2,1)} %bitcast.38, bf16[4096,256]{1,0:T(8,128)(2,1)} %bitcast.37, bf16[512,128]{1,0:T(8,128)(2,1)} %pad_maximum_fusion.2.nk_ref, ...), custom_call_target="tpu_custom_call" | custom-call | tf_op jit(solution)/shard_map/pallas_call | solution.py:107
  98.8 4.4 %all-to-all-start.2 = ((bf16[8,64,2048]{2,1,0:T(8,128)(2,1)}), bf16[8,64,2048]{2,1,0:T(8,128)(2,1)S(1)}, u32[]{:S(2)}, u32[]{:S(2)}) async-start(bf16[8,64,2048]{2,1,0:T(8,128)(2,1)} %bitcast.36), calls=%async_computation.2 | async-start | bytes 4194304 | tf_op jit(solution)/shard_map/all_to_all | solution.py:203
  103.4 0.8 copy.21
  104.3 30.0 %all-to-all-done.2 = bf16[8,64,2048]{2,1,0:T(8,128)(2,1)S(1)} async-done(((bf16[8,64,2048]{2,1,0:T(8,128)(2,1)}), bf16[8,64,2048]{2,1,0:T(8,128)(2,1)S(1)}, u32[]{:S(2)}, u32[]{:S(2)}) %all-to-all-start.2) | async-done | bytes 2097184 | tf_op jit(solution)/shard_map/all_to_all | solution.py:203
  134.8 0.9 fusion.2
  (30 shorter events, 0.8 us)
Async XLA Ops:
  0.6 54.4 %copy-start = (bf16[2048,128]{1,0:T(8,128)(2,1)S(1)}, bf16[2048,128]{1,0:T(8,128)(2,1)}, u32[]{:S(2)}) copy-start(bf16[2048,128]{1,0:T(8,128)(2,1)} %param.13) | copy-start | bytes 1572868
  3.1 6.0 %copy-start.9 = (s32[64]{0:T(128)S(1)}, s32[64]{0:T(128)}, u32[]{:S(2)}) copy-start(s32[64]{0:T(128)} %param.21) | copy-start | bytes 772
  3.1 6.1 %copy-start.1 = (bf16[8,16,256]{2,1,0:T(8,128)(2,1)S(1)}, bf16[8,16,256]{2,1,0:T(8,128)(2,1)}, u32[]{:S(2)}) copy-start(bf16[8,16,256]{2,1,0:T(8,128)(2,1)} %param.22) | copy-start | bytes 196612
  3.1 32.3 %all-to-all-start = ((bf16[8,64,2048]{2,1,0:T(8,128)(2,1)}), bf16[8,64,2048]{2,1,0:T(8,128)(2,1)S(1)}, u32[]{:S(2)}, u32[]{:S(2)}) async-start(bf16[8,64,2048]{2,1,0:T(8,128)(2,1)} %shard_map.131), calls=%async_computation | async-start | bytes 4194304 | tf_op jit(solution)/shard_map/all_to_all | solution.py:165
  35.4 53.4 %all-to-all-start.1 = ((bf16[64,16,256]{2,1,0:T(8,128)(2,1)}), bf16[64,16,256]{2,1,0:T(8,128)(2,1)S(1)}, u32[]{:S(2)}, u32[]{:S(2)}) async-start(bf16[64,16,256]{2,1,0:T(8,128)(2,1)} %broadcast_select_fusion), calls=%async_computation.1 | async-start | bytes 1048576 | tf_op jit(solution)/shard_map/all_to_all | solution.py:169
  55.9 16.7 %copy-start.7 = (f32[128]{0:T(128)S(1)}, f32[128]{0:T(128)}, u32[]{:S(2)}) copy-start(f32[128]{0:T(128)} %param.17) | copy-start | bytes 1540
  56.7 17.0 %copy-start.8 = (f32[128]{0:T(128)S(1)}, f32[128]{0:T(128)}, u32[]{:S(2)}) copy-start(f32[128]{0:T(128)} %param.18) | copy-start | bytes 1540
  72.5 5.1 %copy-start.5 = (bf16[2048,128]{1,0:T(8,128)(2,1)S(1)}, bf16[2048,128]{1,0:T(8,128)(2,1)}, u32[]{:S(2)}) copy-start(bf16[2048,128]{1,0:T(8,128)(2,1)} %param.15) | copy-start | bytes 1572868
  88.9 0.8 copy-start.2
  98.8 4.4 %copy-start.3 = (bf16[512,128]{1,0:T(8,128)(2,1)S(1)}, bf16[512,128]{1,0:T(8,128)(2,1)}, u32[]{:S(2)}) copy-start(bf16[512,128]{1,0:T(8,128)(2,1)} %convolution_convert_fusion.nv_ref) | copy-start | bytes 393220
  98.8 35.5 %all-to-all-start.2 = ((bf16[8,64,2048]{2,1,0:T(8,128)(2,1)}), bf16[8,64,2048]{2,1,0:T(8,128)(2,1)S(1)}, u32[]{:S(2)}, u32[]{:S(2)}) async-start(bf16[8,64,2048]{2,1,0:T(8,128)(2,1)} %bitcast.36), calls=%async_computation.2 | async-start | bytes 4194304 | tf_op jit(solution)/shard_map/all_to_all | solution.py:203
  103.3 31.5 %copy-start.4 = (bf16[1,64,2048]{2,1,0:T(8,128)(2,1)S(1)}, bf16[1,64,2048]{2,1,0:T(8,128)(2,1)}, u32[]{:S(2)}) copy-start(bf16[1,64,2048]{2,1,0:T(8,128)(2,1)} %in_ref.1) | copy-start | bytes 786436
  103.3 31.5 %copy-start.6 = (f32[2048]{0:T(1024)S(1)}, f32[2048]{0:T(1024)}, u32[]{:S(2)}) copy-start(f32[2048]{0:T(1024)} %param.19) | copy-start | bytes 24580
